TPU v7x, 512 devices: a whole 4x4x16 slice. The times are simulated.
512 devices in a mesh: dp: 32 (over y, z_lo, core), ctx: 16 (over x, z_hi).
Axes of the slice: x: 4, y: 4, z: 16 (z_hi: 4, z_lo: 4; z = z_hi * 4 + z_lo), core: 2. Of those that a mesh axis runs over, the one named last changes fastest.
Arguments:
- branch_in: bfloat16 [32, 2048, 2816], P('dp', 'ctx'), may hold values from -6 to 6
- cotangent: bfloat16 [32, 2048, 2816], P('dp', 'ctx'), may hold values from -6 to 6
- weight_a: bfloat16 [256, 2816], P('dp', 'ctx'), may hold values from -0.375 to 0.375
- weight_x: bfloat16 [256, 2816], P('dp', 'ctx'), may hold values from -0.375 to 0.375
- conv_weight: bfloat16 [4, 2816], P(None, 'ctx'), may hold values from -3 to 3
- conv_bias: bfloat16 [2816], P('ctx'), may hold values from -3 to 3
- bias_a: bfloat16 [2816], P('ctx'), may hold values from -4 to 4
- bias_x: bfloat16 [2816], P('ctx'), may hold values from -4 to 4
- rate: bfloat16 [2816], P('ctx'), may hold values from 0 to 0.016, as said below
Outputs:
- grad_input: bfloat16 [32, 2048, 2816], P('dp', 'ctx')
- grad_weight_a: float32 [256, 2816], P('dp', 'ctx')
- grad_rate: float32 [2816], replicated
Inputs may be any that keep to these rules, and one draw needn't show every extreme that they name: `rate`: positive in every channel.
All inputs are finite; a program needn't handle non-finite values.
Results may differ from a plain program's by a relative error of at most 0.006.
Values may be sent and summed in bfloat16 or wider, within the bound.
No kernel may reach another device: no remote copies, remote signals or barrier semaphores. Data moves between devices by JAX's collectives and lax.ppermute only.
A program may use at most 128 MiB of HBM per device.

v0:
```python
import math

import jax
import jax.numpy as jnp
from jax import lax
from jax.sharding import PartitionSpec as P

floor_value = 2.5e-07


def passed_along(array, axis, by):
    length = lax.axis_size(axis)
    pairs = [(i, i + by) for i in range(length) if 0 <= i + by < length]
    return lax.ppermute(array, axis, pairs)


def mix_heads(values, weights):
    tokens = values.shape[0]
    head_width = weights.shape[0]
    head_count = weights.shape[1] // head_width
    left = values.reshape(tokens, head_count, head_width)
    right = weights.reshape(head_width, head_count, head_width)
    result = jnp.einsum("thk,khj->thj", left, right, preferred_element_type=jnp.float32)
    return result.reshape(tokens, head_count * head_width)


def back_heads(grads, weights):
    tokens = grads.shape[0]
    head_width = weights.shape[0]
    head_count = weights.shape[1] // head_width
    left = grads.reshape(tokens, head_count, head_width)
    right = weights.reshape(head_width, head_count, head_width)
    result = jnp.einsum("thj,khj->thk", left, right, preferred_element_type=jnp.float32)
    return result.reshape(tokens, head_count * head_width)


def grad_heads(values, grads, head_width):
    tokens = values.shape[0]
    head_count = values.shape[1] // head_width
    left = values.reshape(tokens, head_count, head_width)
    right = grads.reshape(tokens, head_count, head_width)
    result = jnp.einsum("thk,thj->khj", left, right, preferred_element_type=jnp.float32)
    return result.reshape(head_width, head_count * head_width)


def combine(earlier, later):
    return (earlier[0] * later[0], later[0] * earlier[1] + later[1])


def block_scan(coef, value, reverse):
    length = coef.shape[0]
    width = coef.shape[1]
    block_size = math.gcd(length, 16)
    block_count = length // block_size
    coef_blocks = coef.reshape(block_count, block_size, width)
    value_blocks = value.reshape(block_count, block_size, width)
    visit_order = list(range(block_size))
    if reverse:
        visit_order = visit_order[::-1]
    coef_rows = [None] * block_size
    value_rows = [None] * block_size
    running_coef = None
    running_value = None
    for position in visit_order:
        step_coef = coef_blocks[:, position]
        step_value = value_blocks[:, position]
        if running_coef is None:
            running_coef = step_coef
            running_value = step_value
        else:
            running_value = step_coef * running_value + step_value
            running_coef = running_coef * step_coef
        coef_rows[position] = running_coef
        value_rows[position] = running_value
    local_coef = jnp.stack(coef_rows, 1)
    local_value = jnp.stack(value_rows, 1)
    edge = 0 if reverse else block_size - 1
    summary_coef = local_coef[:, edge]
    summary_value = local_value[:, edge]
    incl_coef, incl_value = lax.associative_scan(
        combine, (summary_coef, summary_value), reverse=reverse, axis=0
    )
    ones_row = jnp.ones((1, width), jnp.float32)
    zero_row = jnp.zeros((1, width), jnp.float32)
    if reverse:
        prior_coef = jnp.concatenate([incl_coef[1:], ones_row], 0)
        prior_value = jnp.concatenate([incl_value[1:], zero_row], 0)
    else:
        prior_coef = jnp.concatenate([ones_row, incl_coef[:-1]], 0)
        prior_value = jnp.concatenate([zero_row, incl_value[:-1]], 0)
    whole_coef = local_coef * prior_coef[:, None]
    whole_value = local_coef * prior_value[:, None] + local_value
    return (whole_coef.reshape(length, width), whole_value.reshape(length, width))


def on_device(
    branch_in, cotangent, weight_a, weight_x, conv_weight, conv_bias, bias_a, bias_x, rate
):
    inputs = branch_in[0]
    upstream = cotangent[0].astype(jnp.float32)
    length = inputs.shape[0]
    taps = conv_weight.shape[0]
    packed = jnp.concatenate(
        [conv_weight, conv_bias[None], bias_a[None], bias_x[None], rate[None]], 0
    )
    rows_a, rows_x = (
        lax.all_gather(weight_a, "dp", axis=0, tiled=True),
        lax.all_gather(weight_x, "dp", axis=0, tiled=True),
    )
    full_a, full_x, params = (
        lax.all_gather(rows_a, "ctx", axis=1, tiled=True),
        lax.all_gather(rows_x, "ctx", axis=1, tiled=True),
        lax.all_gather(packed, "ctx", axis=1, tiled=True),
    )
    params = params.astype(jnp.float32)
    taps_f = params[:taps]
    cbias = params[taps]
    abias = params[taps + 1]
    xbias = params[taps + 2]
    rates = params[taps + 3]
    width = params.shape[1]
    head_width = full_a.shape[0]
    tail = passed_along(inputs[length - (taps - 1) :], "ctx", 1)
    padded = jnp.concatenate([tail, inputs], 0).astype(jnp.float32)
    conv = cbias
    for tap in range(taps):
        conv = conv + taps_f[tap] * padded[tap : tap + length]
    conv_b = conv.astype(jnp.bfloat16)
    conv_f = conv_b.astype(jnp.float32)
    recur_gate = jax.nn.sigmoid(mix_heads(conv_b, full_a) + abias)
    input_gate = jax.nn.sigmoid(mix_heads(conv_b, full_x) + xbias)
    log_decay = -8.0 * recur_gate * rates
    decay = jnp.exp(log_decay)
    one_minus = -jnp.expm1(2.0 * log_decay)
    multiplier = jnp.sqrt(jnp.maximum(one_minus, floor_value))
    drive = multiplier * input_gate * conv_f
    cum_decay, local_hidden = block_scan(decay, drive, False)
    zero_row = jnp.zeros((width,), jnp.float32)
    span = lax.axis_size("ctx")

    def forward_turn(turn, incoming):
        outgoing = cum_decay[-1] * incoming + local_hidden[-1]
        return passed_along(outgoing, "ctx", 1)

    state_in = lax.fori_loop(0, span - 1, forward_turn, zero_row)
    hidden = local_hidden + cum_decay * state_in
    previous = jnp.concatenate([state_in[None], hidden[:-1]], 0)
    coefs = jnp.concatenate([decay[1:], jnp.ones((1, width), jnp.float32)], 0)
    cum_coef, local_back = block_scan(coefs, upstream, True)
    head_coef = decay[0] * cum_coef[0]
    head_value = decay[0] * local_back[0]

    def backward_turn(turn, incoming):
        outgoing = head_coef * incoming + head_value
        return passed_along(outgoing, "ctx", -1)

    back_in = lax.fori_loop(0, span - 1, backward_turn, zero_row)
    back = local_back + cum_coef * back_in
    slope = jnp.where(one_minus > floor_value, 0.5 / multiplier, 0.0)
    d_mult = back * input_gate * conv_f
    d_log = back * previous * decay - 2.0 * decay * decay * d_mult * slope
    d_recur = (d_log * (-8.0 * rates) * recur_gate * (1.0 - recur_gate)).astype(jnp.bfloat16)
    d_input = (back * multiplier * conv_f * input_gate * (1.0 - input_gate)).astype(jnp.bfloat16)
    d_conv = (
        back * multiplier * input_gate + back_heads(d_recur, full_a) + back_heads(d_input, full_x)
    )
    following = passed_along(d_conv[: taps - 1], "ctx", -1)
    dpad = jnp.concatenate([d_conv, following], 0)
    grad_in = jnp.zeros((length, width), jnp.float32)
    for tap in range(taps):
        start = taps - 1 - tap
        grad_in = grad_in + taps_f[tap] * dpad[start : start + length]
    local_wgrad = grad_heads(conv_b, d_recur, head_width)
    row_part = lax.psum_scatter(local_wgrad, "dp", scatter_dimension=0, tiled=True)
    wgrad = lax.psum_scatter(row_part, "ctx", scatter_dimension=1, tiled=True)
    rgrad = lax.psum(jnp.sum(d_log * (-8.0 * recur_gate), axis=0), ("dp", "ctx"))
    return (grad_in.astype(jnp.bfloat16)[None], wgrad, rgrad)


def solution(mesh):
    placed = (
        P("dp", "ctx", None),
        P("dp", "ctx", None),
        P("dp", "ctx"),
        P("dp", "ctx"),
        P(None, "ctx"),
        P("ctx"),
        P("ctx"),
        P("ctx"),
        P("ctx"),
    )
    return jax.shard_map(
        on_device,
        mesh=mesh,
        in_specs=placed,
        out_specs=(P("dp", "ctx", None), P("dp", "ctx"), P()),
        check_vma=False,
    )
```

profile of v0, /device:TPU:6, one launch (start us, length us, event | category | flops | bytes accessed | tf_op | source)
XLA Modules:
  0.0 1051.1 jit_solution(17856726429922451769)
XLA Ops:
  7.2 45.5 %all_gather.16 = bf16[256,176]{1,0:T(8,128)(2,1)S(1)} all-gather(bf16[8,176]{1,0:T(8,128)(2,1)} %param.15), channel_id=1, replica_groups=mesh['dp'=32,'ctx'=16] {'dp'}, dimensions={0}, use_global_device_ids=true | all-gather | bytes 92928 | tf_op jit(solution)/shard_map/all_gather | solution.py:107
  54.3 9.1 collective-permute-start.2
  63.4 38.8 %all_gather.18 = bf16[256,176]{1,0:T(8,128)(2,1)S(1)} all-gather(bf16[8,176]{1,0:T(8,128)(2,1)} %param.16), channel_id=1, replica_groups=mesh['dp'=32,'ctx'=16] {'dp'}, dimensions={0}, use_global_device_ids=true | all-gather | bytes 92928 | tf_op jit(solution)/shard_map/all_gather | solution.py:108
  106.4 51.1 %all-gather = bf16[16,176,8]{1,2,0:T(8,128)(2,1)S(1)} all-gather(bf16[1,176,8]{1,2,0:T(8,128)(2,1)S(1)} %bitcast.278), channel_id=1, replica_groups=mesh['dp'=32,'ctx'=16] {'ctx'}, dimensions={0}, use_global_device_ids=true | all-gather | bytes 47872 | tf_op jit(solution)/shard_map/all_gather | solution.py:113
  187.6 31.9 %all-gather.6.cloned.1.call-done = bf16[256,2816]{0,1:T(8,128)(2,1)} async-done(((bf16[256,176]{0,1:T(8,128)(2,1)}), bf16[256,2816]{0,1:T(8,128)(2,1)}) %all-gather.6.cloned.1.call-update) | async-done | bytes 1441808 | tf_op jit(solution)/shard_map/all_gather | solution.py:112
  225.9 8.2 convert_multiply_fusion.2
  236.9 7.6 fusion.70
  269.7 10.1 slice.532
  279.8 10.1 slice.525
  289.8 10.1 slice.529
  299.9 10.1 slice.527
  391.4 183.0 %while.21 = (s32[]{:T(128)}, f32[2816]{0:T(1024)S(1)}, f32[128,2816]{1,0:T(8,128)}, f32[128,2816]{1,0:T(8,128)}, s32[]{:T(128)}) while((s32[]{:T(128)}, f32[2816]{0:T(1024)S(1)}, f32[128,2816]{1,0:T(8,128)}, f32[128,2816]{1,0:T(8,128)}, s32[]{:T(128)}) %tuple.181), condition=%wide.region_3.0_spmd, body=%wide.region_2.0_spmd.sunk | while | flops 5634 | bytes 135269 | solution.py:145
  397.0 6.6 collective-permute-done.1
  408.3 7.5 collective-permute-done.1
  419.6 8.4 collective-permute-done.1
  431.5 8.7 collective-permute-done.1
  443.7 8.7 collective-permute-done.1
  455.9 8.7 collective-permute-done.1
  468.1 8.7 collective-permute-done.1
  480.3 8.7 collective-permute-done.1
  492.6 8.7 collective-permute-done.1
  504.8 8.7 collective-permute-done.1
  516.9 8.7 collective-permute-done.1
  529.1 8.7 collective-permute-done.1
  541.3 8.7 collective-permute-done.1
  553.5 8.7 collective-permute-done.1
  565.7 8.7 collective-permute-done.1
  611.4 148.9 %while.20 = (s32[]{:T(128)}, f32[2816]{0:T(1024)S(1)}, f32[2816]{0:T(1024)S(1)}, f32[2816]{0:T(1024)S(1)}, s32[]{:T(128)}) while((s32[]{:T(128)}, f32[2816]{0:T(1024)S(1)}, f32[2816]{0:T(1024)S(1)}, f32[2816]{0:T(1024)S(1)}, s32[]{:T(128)}) %tuple.169), condition=%wide.region_1.0_spmd, body=%wide.region_0.0_spmd.sunk | while | flops 5634 | bytes 90213 | solution.py:157
  613.4 7.6 collective-permute-done
  623.9 6.6 collective-permute-done
  634.3 5.7 collective-permute-done
  649.4 5.6 collective-permute-start
  658.9 6.5 collective-permute-start
  668.4 7.4 collective-permute-start
  677.9 8.3 collective-permute-start
  687.6 9.0 collective-permute-start
  698.0 9.0 collective-permute-start
  708.4 9.0 collective-permute-start
  718.8 9.0 collective-permute-start
  729.2 9.0 collective-permute-start
  739.6 9.0 collective-permute-start
  750.0 9.0 collective-permute-start
  760.4 8.9 multiply_reduce_fusion
  788.1 9.0 collective-permute-start.3
  797.1 100.7 %psum.7 = f32[2816]{0:T(1024)} all-reduce(f32[2816]{0:T(1024)S(1)} %get-tuple-element.94), channel_id=1, replica_groups=mesh['dp'=32,'ctx'=16] {'dp','ctx'}, use_global_device_ids=true, to_apply=%region_7.8 | all-reduce | flops 2816 | bytes 22528 | tf_op jit(solution)/shard_map/psum | solution.py:176
  898.3 28.1 %reduce-scatter.5.cloned.1.call-done = f32[8,2816]{1,0:T(8,128)} async-done(((f32[256,2816]{1,0:T(8,128)}), f32[8,2816]{1,0:T(8,128)}) %reduce-scatter.5.cloned.1.call-update) | async-done | bytes 90128 | tf_op jit(solution)/shard_map/reduce_scatter | solution.py:174
  928.9 4.8 fusion.38
  935.9 107.1 %reduce-scatter.7.cloned.1.call-done = f32[176,8]{1,0:T(8,128)} async-done(((f32[2816,8]{1,0:T(8,128)}), f32[176,8]{1,0:T(8,128)}) %reduce-scatter.7.cloned.1.call-update) | async-done | bytes 5648
  (468 shorter events, 307.4 us)
Async XLA Ops:
  7.2 150.5 %copy-start.14 = (bf16[1,128,2816]{2,1,0:T(8,128)(2,1)S(1)}, bf16[1,128,2816]{2,1,0:T(8,128)(2,1)}, u32[]{:S(2)}) copy-start(bf16[1,128,2816]{2,1,0:T(8,128)(2,1)} %param.14) | copy-start | bytes 2162692
  7.2 161.4 %all-gather.4.cloned.1.call-start = ((), (), s32[]{:S(2)}) async-start(), calls=%async_computation.2 | async-start | bytes 1531904 | tf_op jit(solution)/shard_map/all_gather | solution.py:111
  53.5 166.1 %all-gather.6.cloned.1.call-start = ((), (), s32[]{:S(2)}) async-start(), calls=%async_computation.3 | async-start | bytes 1531904 | tf_op jit(solution)/shard_map/all_gather | solution.py:112
  54.3 106.7 %collective-permute-start.2 = (bf16[3,2816]{1,0:T(4,128)(2,1)S(1)}, bf16[3,2816]{1,0:T(4,128)(2,1)S(1)}, u32[]{:S(2)}, u32[]{:S(2)}) collective-permute-start(bf16[3,2816]{1,0:T(4,128)(2,1)S(1)} %slice_bitcast_fusion), channel_id=1, source_target_pairs={{0,1},{1,2},{2,3},{3,4},{4,5},{5,6},{6,7},{7,8},{8,9},{9,10},{10,1... | collective-permute-start | bytes 50696 | tf_op jit(solution)/shard_map/ppermute | solution.py:14
  103.0 823.4 %reduce-scatter.5.cloned.1.call-start = ((), (), s32[]{:S(2)}) async-start(), calls=%async_computation.4 | async-start | bytes 2973696 | tf_op jit(solution)/shard_map/reduce_scatter | solution.py:174
  159.8 66.0 %copy-start.77 = (f32[2816]{0:T(1024)}, f32[2816]{0:T(1024)S(1)}, u32[]{:S(2)}) copy-start(f32[2816]{0:T(1024)S(1)} %get-tuple-element.73) | copy-start | bytes 33796
  159.8 66.0 %copy-start.79 = (f32[2816]{0:T(1024)}, f32[2816]{0:T(1024)S(1)}, u32[]{:S(2)}) copy-start(f32[2816]{0:T(1024)S(1)} %get-tuple-element.74) | copy-start | bytes 33796
  159.9 66.0 %copy-start.81 = (f32[2816]{0:T(1024)}, f32[2816]{0:T(1024)S(1)}, u32[]{:S(2)}) copy-start(f32[2816]{0:T(1024)S(1)} %get-tuple-element.75) | copy-start | bytes 33796
  159.9 66.0 %copy-start.83 = (f32[2816]{0:T(1024)}, f32[2816]{0:T(1024)S(1)}, u32[]{:S(2)}) copy-start(f32[2816]{0:T(1024)S(1)} %get-tuple-element.77) | copy-start | bytes 33796
  159.9 66.0 %copy-start.85 = (f32[2816]{0:T(1024)}, f32[2816]{0:T(1024)S(1)}, u32[]{:S(2)}) copy-start(f32[2816]{0:T(1024)S(1)} %get-tuple-element.76) | copy-start | bytes 33796
  393.0 10.6 %collective-permute-start.1 = (f32[2816]{0:T(1024)}, f32[2816]{0:T(1024)S(1)}, u32[]{:S(2)}, u32[]{:S(2)}) collective-permute-start(f32[2816]{0:T(1024)} %multiply_add_fusion.31), channel_id=1, source_target_pairs={{0,1},{1,2},{2,3},{3,4},{4,5},{5,6},{6,7},{7,8},{8,9},{9,10},{10,1... | collective-permute-start | bytes 33800 | tf_op jit(solution)/shard_map/while/body/eval_jaxpr/ppermute | solution.py:14
  405.2 10.6 %collective-permute-start.1 = (f32[2816]{0:T(1024)}, f32[2816]{0:T(1024)S(1)}, u32[]{:S(2)}, u32[]{:S(2)}) collective-permute-start(f32[2816]{0:T(1024)} %multiply_add_fusion.31), channel_id=1, source_target_pairs={{0,1},{1,2},{2,3},{3,4},{4,5},{5,6},{6,7},{7,8},{8,9},{9,10},{10,1... | collective-permute-start | bytes 33800 | tf_op jit(solution)/shard_map/while/body/eval_jaxpr/ppermute | solution.py:14
  417.4 10.6 %collective-permute-start.1 = (f32[2816]{0:T(1024)}, f32[2816]{0:T(1024)S(1)}, u32[]{:S(2)}, u32[]{:S(2)}) collective-permute-start(f32[2816]{0:T(1024)} %multiply_add_fusion.31), channel_id=1, source_target_pairs={{0,1},{1,2},{2,3},{3,4},{4,5},{5,6},{6,7},{7,8},{8,9},{9,10},{10,1... | collective-permute-start | bytes 33800 | tf_op jit(solution)/shard_map/while/body/eval_jaxpr/ppermute | solution.py:14
  429.6 10.6 %collective-permute-start.1 = (f32[2816]{0:T(1024)}, f32[2816]{0:T(1024)S(1)}, u32[]{:S(2)}, u32[]{:S(2)}) collective-permute-start(f32[2816]{0:T(1024)} %multiply_add_fusion.31), channel_id=1, source_target_pairs={{0,1},{1,2},{2,3},{3,4},{4,5},{5,6},{6,7},{7,8},{8,9},{9,10},{10,1... | collective-permute-start | bytes 33800 | tf_op jit(solution)/shard_map/while/body/eval_jaxpr/ppermute | solution.py:14
  441.8 10.6 %collective-permute-start.1 = (f32[2816]{0:T(1024)}, f32[2816]{0:T(1024)S(1)}, u32[]{:S(2)}, u32[]{:S(2)}) collective-permute-start(f32[2816]{0:T(1024)} %multiply_add_fusion.31), channel_id=1, source_target_pairs={{0,1},{1,2},{2,3},{3,4},{4,5},{5,6},{6,7},{7,8},{8,9},{9,10},{10,1... | collective-permute-start | bytes 33800 | tf_op jit(solution)/shard_map/while/body/eval_jaxpr/ppermute | solution.py:14
  454.0 10.6 %collective-permute-start.1 = (f32[2816]{0:T(1024)}, f32[2816]{0:T(1024)S(1)}, u32[]{:S(2)}, u32[]{:S(2)}) collective-permute-start(f32[2816]{0:T(1024)} %multiply_add_fusion.31), channel_id=1, source_target_pairs={{0,1},{1,2},{2,3},{3,4},{4,5},{5,6},{6,7},{7,8},{8,9},{9,10},{10,1... | collective-permute-start | bytes 33800 | tf_op jit(solution)/shard_map/while/body/eval_jaxpr/ppermute | solution.py:14
  466.2 10.6 %collective-permute-start.1 = (f32[2816]{0:T(1024)}, f32[2816]{0:T(1024)S(1)}, u32[]{:S(2)}, u32[]{:S(2)}) collective-permute-start(f32[2816]{0:T(1024)} %multiply_add_fusion.31), channel_id=1, source_target_pairs={{0,1},{1,2},{2,3},{3,4},{4,5},{5,6},{6,7},{7,8},{8,9},{9,10},{10,1... | collective-permute-start | bytes 33800 | tf_op jit(solution)/shard_map/while/body/eval_jaxpr/ppermute | solution.py:14
  478.4 10.6 %collective-permute-start.1 = (f32[2816]{0:T(1024)}, f32[2816]{0:T(1024)S(1)}, u32[]{:S(2)}, u32[]{:S(2)}) collective-permute-start(f32[2816]{0:T(1024)} %multiply_add_fusion.31), channel_id=1, source_target_pairs={{0,1},{1,2},{2,3},{3,4},{4,5},{5,6},{6,7},{7,8},{8,9},{9,10},{10,1... | collective-permute-start | bytes 33800 | tf_op jit(solution)/shard_map/while/body/eval_jaxpr/ppermute | solution.py:14
  490.6 10.6 %collective-permute-start.1 = (f32[2816]{0:T(1024)}, f32[2816]{0:T(1024)S(1)}, u32[]{:S(2)}, u32[]{:S(2)}) collective-permute-start(f32[2816]{0:T(1024)} %multiply_add_fusion.31), channel_id=1, source_target_pairs={{0,1},{1,2},{2,3},{3,4},{4,5},{5,6},{6,7},{7,8},{8,9},{9,10},{10,1... | collective-permute-start | bytes 33800 | tf_op jit(solution)/shard_map/while/body/eval_jaxpr/ppermute | solution.py:14
  502.8 10.6 %collective-permute-start.1 = (f32[2816]{0:T(1024)}, f32[2816]{0:T(1024)S(1)}, u32[]{:S(2)}, u32[]{:S(2)}) collective-permute-start(f32[2816]{0:T(1024)} %multiply_add_fusion.31), channel_id=1, source_target_pairs={{0,1},{1,2},{2,3},{3,4},{4,5},{5,6},{6,7},{7,8},{8,9},{9,10},{10,1... | collective-permute-start | bytes 33800 | tf_op jit(solution)/shard_map/while/body/eval_jaxpr/ppermute | solution.py:14
  515.0 10.6 %collective-permute-start.1 = (f32[2816]{0:T(1024)}, f32[2816]{0:T(1024)S(1)}, u32[]{:S(2)}, u32[]{:S(2)}) collective-permute-start(f32[2816]{0:T(1024)} %multiply_add_fusion.31), channel_id=1, source_target_pairs={{0,1},{1,2},{2,3},{3,4},{4,5},{5,6},{6,7},{7,8},{8,9},{9,10},{10,1... | collective-permute-start | bytes 33800 | tf_op jit(solution)/shard_map/while/body/eval_jaxpr/ppermute | solution.py:14
  527.2 10.6 %collective-permute-start.1 = (f32[2816]{0:T(1024)}, f32[2816]{0:T(1024)S(1)}, u32[]{:S(2)}, u32[]{:S(2)}) collective-permute-start(f32[2816]{0:T(1024)} %multiply_add_fusion.31), channel_id=1, source_target_pairs={{0,1},{1,2},{2,3},{3,4},{4,5},{5,6},{6,7},{7,8},{8,9},{9,10},{10,1... | collective-permute-start | bytes 33800 | tf_op jit(solution)/shard_map/while/body/eval_jaxpr/ppermute | solution.py:14
  539.4 10.6 %collective-permute-start.1 = (f32[2816]{0:T(1024)}, f32[2816]{0:T(1024)S(1)}, u32[]{:S(2)}, u32[]{:S(2)}) collective-permute-start(f32[2816]{0:T(1024)} %multiply_add_fusion.31), channel_id=1, source_target_pairs={{0,1},{1,2},{2,3},{3,4},{4,5},{5,6},{6,7},{7,8},{8,9},{9,10},{10,1... | collective-permute-start | bytes 33800 | tf_op jit(solution)/shard_map/while/body/eval_jaxpr/ppermute | solution.py:14
  551.6 10.6 %collective-permute-start.1 = (f32[2816]{0:T(1024)}, f32[2816]{0:T(1024)S(1)}, u32[]{:S(2)}, u32[]{:S(2)}) collective-permute-start(f32[2816]{0:T(1024)} %multiply_add_fusion.31), channel_id=1, source_target_pairs={{0,1},{1,2},{2,3},{3,4},{4,5},{5,6},{6,7},{7,8},{8,9},{9,10},{10,1... | collective-permute-start | bytes 33800 | tf_op jit(solution)/shard_map/while/body/eval_jaxpr/ppermute | solution.py:14
  563.8 10.6 %collective-permute-start.1 = (f32[2816]{0:T(1024)}, f32[2816]{0:T(1024)S(1)}, u32[]{:S(2)}, u32[]{:S(2)}) collective-permute-start(f32[2816]{0:T(1024)} %multiply_add_fusion.31), channel_id=1, source_target_pairs={{0,1},{1,2},{2,3},{3,4},{4,5},{5,6},{6,7},{7,8},{8,9},{9,10},{10,1... | collective-permute-start | bytes 33800 | tf_op jit(solution)/shard_map/while/body/eval_jaxpr/ppermute | solution.py:14
  610.6 149.8 %copy-start.78 = (f32[2816]{0:T(1024)S(1)}, f32[2816]{0:T(1024)}, u32[]{:S(2)}) copy-start(f32[2816]{0:T(1024)} %copy-done.77) | copy-start | bytes 33796
  610.6 149.8 %copy-start.80 = (f32[2816]{0:T(1024)S(1)}, f32[2816]{0:T(1024)}, u32[]{:S(2)}) copy-start(f32[2816]{0:T(1024)} %copy-done.79) | copy-start | bytes 33796
  610.6 149.8 %copy-start.82 = (f32[2816]{0:T(1024)S(1)}, f32[2816]{0:T(1024)}, u32[]{:S(2)}) copy-start(f32[2816]{0:T(1024)} %copy-done.81) | copy-start | bytes 33796
  610.6 149.8 %copy-start.84 = (f32[2816]{0:T(1024)S(1)}, f32[2816]{0:T(1024)}, u32[]{:S(2)}) copy-start(f32[2816]{0:T(1024)} %copy-done.83) | copy-start | bytes 33796
  610.6 149.8 %copy-start.86 = (f32[2816]{0:T(1024)S(1)}, f32[2816]{0:T(1024)}, u32[]{:S(2)}) copy-start(f32[2816]{0:T(1024)} %copy-done.85) | copy-start | bytes 33796
  610.6 149.8 %copy-start.88 = (f32[2816]{0:T(1024)S(1)}, f32[2816]{0:T(1024)}, u32[]{:S(2)}) copy-start(f32[2816]{0:T(1024)} %copy-done.87) | copy-start | bytes 33796
  611.5 9.5 collective-permute-start
  621.0 9.5 collective-permute-start
  630.5 9.5 collective-permute-start
  640.0 9.5 collective-permute-start
  649.4 9.5 collective-permute-start
  658.9 9.5 collective-permute-start
  668.4 9.5 collective-permute-start
  677.9 9.7 collective-permute-start
  687.6 10.4 collective-permute-start
  698.0 10.4 collective-permute-start
  708.4 10.4 collective-permute-start
  718.8 10.4 collective-permute-start
  729.2 10.4 collective-permute-start
  739.6 10.4 collective-permute-start
  750.0 10.4 collective-permute-start
  774.0 269.0 %reduce-scatter.7.cloned.1.call-start = ((), (), s32[]{:S(2)}) async-start(), calls=%async_computation.5 | async-start | bytes 1531904
  788.1 109.7 %collective-permute-start.3 = (f32[3,2816]{1,0:T(4,128)S(1)}, f32[3,2816]{1,0:T(4,128)S(1)}, u32[]{:S(2)}, u32[]{:S(2)}) collective-permute-start(f32[3,2816]{1,0:T(4,128)S(1)} %copy.775), channel_id=1, source_target_pairs={{1,0},{2,1},{3,2},{4,3},{5,4},{6,5},{7,6},{8,7},{9,8},{10,9},{11,1... | collective-permute-start | bytes 101384 | tf_op jit(solution)/shard_map/ppermute | solution.py:14
  (85 other events, 391.6 us)
Sparse Core Ops, SparseCore 0:
  53.6 84.7 all-gather.3
  141.4 78.0 all-gather.5
  774.2 152.1 reduce-scatter.4
  930.3 112.6 reduce-scatter.6
where the time goes:
time: 1060 us; the launch traced here: 1050 us
  waiting for transfers between devices  338 us (32%)
  blocking collectives  236 us (22%)
  local copies, waits for them, and re-layouts  192 us (18%)
  starting transfers between devices  155 us (15%)
  other arithmetic  104 us (10%)
  between operations  14.9 us (1%)
    ppermute x32, waiting for transfers between devices, passed_along(): return lax.ppermute(array, axis, pairs)  171 us
    ppermute x32, starting transfers between devices, passed_along(): return lax.ppermute(array, axis, pairs)  154 us
    unnamed x5, waiting for transfers between devices  107 us
    psum x1, blocking collectives, on_device(): lax.psum(jnp.sum(d_log * (-8.0 * recur_gate), axis=0), ('dp', 'ctx'))  101 us
    slice x30, local copies, waits for them, and re-layouts, block_scan(): lax.associative_scan(combine, (summary_coef, summary_value), reverse=reve...  62.1 us
    all_gather x1, blocking collectives, on_device(): lax.all_gather(packed, 'ctx', axis=1, tiled=True)  51.1 us
    all_gather x1, blocking collectives, on_device(): lax.all_gather(weight_a, 'dp', axis=0, tiled=True)  45.5 us
    all_gather x1, blocking collectives, on_device(): lax.all_gather(weight_x, 'dp', axis=0, tiled=True)  38.8 us
  transfers between devices with their start and end apart: 36, of which 33 were waited for; matrix products, arithmetic and copies ran while one was open for 5% of the time, Pallas kernels for 0%

commit v1 on v0

v1 whole, which is shorter than its diff:
```python
import jax
import jax.numpy as jnp
from jax import lax
from jax.sharding import PartitionSpec as P

floor_value = 2.5e-07
exact = lax.Precision.HIGHEST


def passed_along(array, axis, by):
    length = lax.axis_size(axis)
    pairs = [(i, i + by) for i in range(length) if 0 <= i + by < length]
    return lax.ppermute(array, axis, pairs)


def mix_heads(values, weights):
    tokens = values.shape[0]
    head_width = weights.shape[0]
    head_count = weights.shape[1] // head_width
    left = values.reshape(tokens, head_count, head_width)
    right = weights.reshape(head_width, head_count, head_width)
    result = jnp.einsum("thk,khj->thj", left, right, preferred_element_type=jnp.float32)
    return result.reshape(tokens, head_count * head_width)


def back_heads(grads, weights):
    tokens = grads.shape[0]
    head_width = weights.shape[0]
    head_count = weights.shape[1] // head_width
    left = grads.reshape(tokens, head_count, head_width)
    right = weights.reshape(head_width, head_count, head_width)
    result = jnp.einsum("thj,khj->thk", left, right, preferred_element_type=jnp.float32)
    return result.reshape(tokens, head_count * head_width)


def grad_heads(values, grads, head_width):
    tokens = values.shape[0]
    head_count = values.shape[1] // head_width
    left = values.reshape(tokens, head_count, head_width)
    right = grads.reshape(tokens, head_count, head_width)
    result = jnp.einsum("thk,thj->khj", left, right, preferred_element_type=jnp.float32)
    return result.reshape(head_width, head_count * head_width)


def compose(own, received):
    return (own[0] * received[0], own[0] * received[1] + own[1])


def block_prefix(forward_item, backward_item, axis):
    span = lax.axis_size(axis)
    ones = jnp.ones_like(forward_item[0])
    zeros = jnp.zeros_like(forward_item[0])
    fwd_incl, fwd_excl = forward_item, (ones, zeros)
    bwd_incl, bwd_excl = backward_item, (ones, zeros)
    shift = 1
    while shift < span:
        got_fwd = passed_along(jnp.stack(fwd_incl), axis, shift)
        got_bwd = passed_along(jnp.stack(bwd_incl), axis, -shift)
        got_fwd = (got_fwd[0], got_fwd[1])
        got_bwd = (got_bwd[0], got_bwd[1])
        fwd_excl = compose(fwd_excl, got_fwd)
        fwd_incl = compose(fwd_incl, got_fwd)
        bwd_excl = compose(bwd_excl, got_bwd)
        bwd_incl = compose(bwd_incl, got_bwd)
        shift *= 2
    return fwd_excl[1], bwd_excl[1]


def on_device(
    branch_in, cotangent, weight_a, weight_x, conv_weight, conv_bias, bias_a, bias_x, rate
):
    inputs = branch_in[0]
    upstream = cotangent[0].astype(jnp.float32)
    length = inputs.shape[0]
    taps = conv_weight.shape[0]
    rows, cols = weight_a.shape
    dp_size = lax.axis_size("dp")
    ctx_size = lax.axis_size("ctx")
    packed = jnp.concatenate(
        [conv_weight, conv_bias[None], bias_a[None], bias_x[None], rate[None]], 0
    )
    param_rows = packed.shape[0]
    both = lax.all_gather(jnp.stack([weight_a, weight_x]), "dp", axis=1, tiled=True)
    head_width = both.shape[1]
    joined = jnp.concatenate([both.reshape(2 * head_width, cols), packed], 0)
    joined = lax.all_gather(joined, "ctx", axis=1, tiled=True)
    full_a = joined[:head_width]
    full_x = joined[head_width : 2 * head_width]
    params = joined[2 * head_width :]
    params = params.astype(jnp.float32)
    taps_f = params[:taps]
    cbias = params[taps]
    abias = params[taps + 1]
    xbias = params[taps + 2]
    rates = params[taps + 3]
    width = params.shape[1]
    tail = passed_along(inputs[length - (taps - 1) :], "ctx", 1)
    padded = jnp.concatenate([tail, inputs], 0).astype(jnp.float32)
    conv = cbias
    for tap in range(taps):
        conv = conv + taps_f[tap] * padded[tap : tap + length]
    conv_b = conv.astype(jnp.bfloat16)
    conv_f = conv_b.astype(jnp.float32)
    recur_gate = jax.nn.sigmoid(mix_heads(conv_b, full_a) + abias)
    input_gate = jax.nn.sigmoid(mix_heads(conv_b, full_x) + xbias)
    log_decay = -8.0 * recur_gate * rates
    decay = jnp.exp(log_decay)
    one_minus = -jnp.expm1(2.0 * log_decay)
    multiplier = jnp.sqrt(jnp.maximum(one_minus, floor_value))
    drive = multiplier * input_gate * conv_f

    row_id = lax.broadcasted_iota(jnp.int32, (length, length), 0)
    col_id = lax.broadcasted_iota(jnp.int32, (length, length), 1)
    lower = (row_id >= col_id).astype(jnp.float32)
    upper = (row_id <= col_id).astype(jnp.float32)
    cum_log = jnp.dot(lower, log_decay, precision=exact)
    grow = jnp.exp(cum_log)
    shrink = jnp.exp(-cum_log)
    local_hidden = grow * jnp.dot(lower, shrink * drive, precision=exact)
    weighted_back = jnp.dot(upper, grow * upstream, precision=exact)
    local_back = shrink * weighted_back
    block_decay = grow[-1]
    state_in, back_in = block_prefix(
        (block_decay, local_hidden[-1]), (block_decay, weighted_back[0]), "ctx"
    )
    hidden = local_hidden + grow * state_in
    previous = jnp.concatenate([state_in[None], hidden[:-1]], 0)
    back = local_back + (block_decay * shrink) * back_in
    slope = jnp.where(one_minus > floor_value, 0.5 / multiplier, 0.0)
    d_mult = back * input_gate * conv_f
    d_log = back * previous * decay - 2.0 * decay * decay * d_mult * slope
    d_recur = (d_log * (-8.0 * rates) * recur_gate * (1.0 - recur_gate)).astype(jnp.bfloat16)
    d_input = (back * multiplier * conv_f * input_gate * (1.0 - input_gate)).astype(jnp.bfloat16)
    d_conv = (
        back * multiplier * input_gate + back_heads(d_recur, full_a) + back_heads(d_input, full_x)
    )
    following = passed_along(d_conv[: taps - 1], "ctx", -1)
    dpad = jnp.concatenate([d_conv, following], 0)
    grad_in = jnp.zeros((length, width), jnp.float32)
    for tap in range(taps):
        start = taps - 1 - tap
        grad_in = grad_in + taps_f[tap] * dpad[start : start + length]
    local_wgrad = grad_heads(conv_b, d_recur, head_width)
    row_part = lax.psum_scatter(local_wgrad, "dp", scatter_dimension=0, tiled=True)
    wgrad = lax.psum_scatter(row_part, "ctx", scatter_dimension=1, tiled=True)
    rgrad = lax.psum(jnp.sum(d_log * (-8.0 * recur_gate), axis=0), ("dp", "ctx"))
    return (grad_in.astype(jnp.bfloat16)[None], wgrad, rgrad)


def solution(mesh):
    placed = (
        P("dp", "ctx", None),
        P("dp", "ctx", None),
        P("dp", "ctx"),
        P("dp", "ctx"),
        P(None, "ctx"),
        P("ctx"),
        P("ctx"),
        P("ctx"),
        P("ctx"),
    )
    return jax.shard_map(
        on_device,
        mesh=mesh,
        in_specs=placed,
        out_specs=(P("dp", "ctx", None), P("dp", "ctx"), P()),
        check_vma=False,
    )
```

time: 1060 us -> 553 us (0.52)
  local copies, waits for them, and re-layouts: 192 us -> 31.8 us
  starting transfers between devices: 155 us -> 53.8 us
  blocking collectives: 236 us -> 148 us
  other arithmetic: 104 us -> 19.2 us
  waiting for transfers between devices: 338 us -> 265 us
    ppermute x32 -> x10, waiting for transfers between devices: 171 us -> 13.4 us  [passed_along(): return lax.ppermute(array, axis, pairs)]
    ppermute x32 -> x10, starting transfers between devices: 154 us -> 53.6 us  [passed_along(): return lax.ppermute(array, axis, pairs)]
    slice x55 -> x4, local copies, waits for them, and re-layouts: 95.7 us -> 3.24 us  [the longest x1 3.21 us: on_device(): full_a = joined[:head_width]]
    all_gather x3 -> x1, blocking collectives: 135 us -> 45.6 us  [on_device(): lax.all_gather(jnp.stack([weight_a, weight_x]), 'dp', axis=1, tiled=True)]
    all_gather x2 -> x1, waiting for transfers between devices: 31.9 us -> 109 us  [on_device(): joined = lax.all_gather(joined, 'ctx', axis=1, tiled=True)]
    unnamed x226 -> x27, local copies, waits for them, and re-layouts: 37.1 us -> 7.07 us
    unnamed x29 -> x0, other arithmetic: 23.8 us -> none
    add x43 -> x3, other arithmetic: 22 us -> 0.3 us  [the longest x2 0.15 us: compose(): return (own[0] * received[0], own[0] * received[1] + own[1])]
  transfers between devices with their start and end apart: 36 -> 13, of which waited for: 33 -> 8; matrix products, arithmetic and copies ran while one was open for 5% -> 3% of each run, Pallas kernels for 0% -> 0%
where the time goes in v1:
time: 553 us; the launch traced here: 550 us
  waiting for transfers between devices  265 us (48%)
  blocking collectives  148 us (27%)
  starting transfers between devices  53.8 us (10%)
  local copies, waits for them, and re-layouts  31.8 us (6%)
  other arithmetic  19.2 us (3%)
  matrix products  18.4 us (3%)
  between operations  14.2 us (3%)
    unnamed x4, waiting for transfers between devices  112 us
    all_gather x1, waiting for transfers between devices, on_device(): joined = lax.all_gather(joined, 'ctx', axis=1, tiled=True)  109 us
    psum x1, blocking collectives, on_device(): lax.psum(jnp.sum(d_log * (-8.0 * recur_gate), axis=0), ('dp', 'ctx'))  102 us
    ppermute x10, starting transfers between devices, passed_along(): return lax.ppermute(array, axis, pairs)  53.6 us
    all_gather x1, blocking collectives, on_device(): lax.all_gather(jnp.stack([weight_a, weight_x]), 'dp', axis=1, tiled=True)  45.6 us
    reduce_scatter x1, waiting for transfers between devices, on_device(): lax.psum_scatter(local_wgrad, 'dp', scatter_dimension=0, tiled=True)  30.2 us
    ppermute x10, waiting for transfers between devices, passed_along(): return lax.ppermute(array, axis, pairs)  13.4 us
  transfers between devices with their start and end apart: 13, of which 8 were waited for; matrix products, arithmetic and copies ran while one was open for 3% of the time, Pallas kernels for 0%

profile of v1, /device:TPU:6, one launch (start us, length us, event | category | flops | bytes accessed | tf_op | source)
XLA Modules:
  0.0 550.1 jit_solution(4851495166393935835)
XLA Ops:
  7.2 0.9 copy.45
  11.8 45.6 %all_gather.6 = bf16[2,256,176]{2,1,0:T(8,128)(2,1)S(1)} all-gather(bf16[2,8,176]{2,1,0:T(8,128)(2,1)S(1)} %pad_maximum_fusion.9), channel_id=1, replica_groups=mesh['dp'=32,'ctx'=16] {'dp'}, dimensions={1}, use_global_device_ids=true | all-gather | bytes 185856 | tf_op jit(solution)/shard_map/all_gather | solution.py:83
  57.6 0.8 concatenate.12
  58.5 9.1 %collective-permute-start = (bf16[3,2816]{1,0:T(4,128)(2,1)S(1)}, bf16[3,2816]{1,0:T(4,128)(2,1)S(1)}, u32[]{:S(2)}, u32[]{:S(2)}) collective-permute-start(bf16[3,2816]{1,0:T(4,128)(2,1)S(1)} %slice_bitcast_fusion), channel_id=1, source_target_pairs={{0,1},{1,2},{2,3},{3,4},{4,5},{5,6},{6,7},{7,8},{8,9},{9,10},{10,1... | collective-permute-start | bytes 50696 | tf_op jit(solution)/shard_map/ppermute | solution.py:13
  67.6 3.1 collective-permute-done
  70.9 109.3 %all-gather.2.cloned.1.call-done = bf16[520,2816]{0,1:T(8,128)(2,1)} async-done(((bf16[520,176]{0,1:T(8,128)(2,1)}), bf16[520,2816]{0,1:T(8,128)(2,1)}) %all-gather.2.cloned.1.call-update) | async-done | bytes 2928656 | tf_op jit(solution)/shard_map/all_gather | solution.py:86
  180.2 1.2 slice_convert_fusion
  181.4 5.7 %slice_reduce_fusion = (f32[2816]{0:T(1024)S(1)}, f32[2816]{0:T(1024)S(1)}, f32[2816]{0:T(1024)S(1)}, f32[2816]{0:T(1024)S(1)}, f32[2816]{0:T(1024)S(1)}, /*inde...) fusion(f32[8,2816]{0,1:T(8,128)S(1)} %slice_convert_fusion), kind=kLoop, calls=%fused_computation.28 | loop fusion | flops 2816 | bytes 180224 | tf_op jit(solution)/shard_map/slice | solution.py:94
  187.7 0.9 copy-done.8
  188.6 1.1 copy.50
  189.7 3.2 fusion.45
  192.9 1.7 fusion.48
  194.6 2.9 copy.54
  197.5 3.2 fusion.47
  200.7 2.9 copy.52
  203.6 2.8 fusion.46
  206.5 2.7 convolution_multiply_fusion
  209.3 1.3 fusion.24
  210.6 5.1 collective-permute-start.5
  215.7 5.6 %collective-permute-start.1 = (f32[2,2816]{1,0:T(2,128)S(1)}, f32[2,2816]{1,0:T(2,128)S(1)}, u32[]{:S(2)}, u32[]{:S(2)}) collective-permute-start(f32[2,2816]{1,0:T(2,128)S(1)} %get-tuple-element.37), channel_id=1, source_target_pairs={{1,0},{2,1},{3,2},{4,3},{5,4},{6,5},{7,6},{8,7},{9,8},{10,9},{11,1... | collective-permute-start | bytes 67592 | tf_op jit(solution)/shard_map/ppermute | solution.py:13
  221.3 4.0 collective-permute-done.1
  225.4 7.3 %collective-permute-start.6 = (f32[2,2816]{1,0:T(2,128)S(1)}, f32[2,2816]{1,0:T(2,128)S(1)}, u32[]{:S(2)}, u32[]{:S(2)}) collective-permute-start(f32[2,2816]{1,0:T(2,128)S(1)} %pad_maximum_fusion.6), channel_id=1, source_target_pairs={{0,2},{1,3},{2,4},{3,5},{4,6},{5,7},{6,8},{7,9},{8,10},{9,11},{10,... | collective-permute-start | bytes 67592 | tf_op jit(solution)/shard_map/ppermute | solution.py:13
  232.8 8.1 %collective-permute-start.2 = (f32[2,2816]{1,0:T(2,128)S(1)}, f32[2,2816]{1,0:T(2,128)S(1)}, u32[]{:S(2)}, u32[]{:S(2)}) collective-permute-start(f32[2,2816]{1,0:T(2,128)S(1)} %pad_maximum_fusion.3), channel_id=1, source_target_pairs={{2,0},{3,1},{4,2},{5,3},{6,4},{7,5},{8,6},{9,7},{10,8},{11,9},{12,... | collective-permute-start | bytes 67592 | tf_op jit(solution)/shard_map/ppermute | solution.py:13
  241.0 1.3 collective-permute-start.7
  242.3 4.9 collective-permute-done.2
  247.3 2.7 collective-permute-start.3
  250.1 1.3 collective-permute-start.8
  251.6 6.0 %collective-permute-start.4 = (f32[2,2816]{1,0:T(2,128)S(1)}, f32[2,2816]{1,0:T(2,128)S(1)}, u32[]{:S(2)}, u32[]{:S(2)}) collective-permute-start(f32[2,2816]{1,0:T(2,128)S(1)} %pad_maximum_fusion.5), channel_id=1, source_target_pairs={{8,0},{9,1},{10,2},{11,3},{12,4},{13,5},{14,6},{15,7},{24,16},{25,... | collective-permute-start | bytes 67592 | tf_op jit(solution)/shard_map/ppermute | solution.py:13
  257.8 1.2 collective-permute-done.4
  259.1 4.6 multiply_reduce_fusion
  263.7 1.3 multiply_convert_fusion
  265.1 1.5 copy.55
  266.6 2.2 fusion.51
  268.8 3.4 copy.64
  272.2 1.3 copy-done
  273.5 2.8 fusion.49
  276.3 3.0 copy.58
  279.3 1.1 copy.59
  280.5 1.7 fusion.50
  282.2 1.5 copy.62
  283.7 2.6 add_add_fusion
  286.4 7.1 %collective-permute-start.9 = (f32[3,2816]{1,0:T(4,128)S(1)}, f32[3,2816]{1,0:T(4,128)S(1)}, u32[]{:S(2)}, u32[]{:S(2)}) collective-permute-start(f32[3,2816]{1,0:T(4,128)S(1)} %slice.199), channel_id=1, source_target_pairs={{1,0},{2,1},{3,2},{4,3},{5,4},{6,5},{7,6},{8,7},{9,8},{10,9},{11,1... | collective-permute-start | bytes 101384 | tf_op jit(solution)/shard_map/ppermute | solution.py:13
  293.5 102.0 %psum.7 = f32[2816]{0:T(1024)} all-reduce(f32[2816]{0:T(1024)S(1)} %get-tuple-element.11), channel_id=1, replica_groups=mesh['dp'=32,'ctx'=16] {'dp','ctx'}, use_global_device_ids=true, to_apply=%region_3.4 | all-reduce | flops 2816 | bytes 22528 | tf_op jit(solution)/shard_map/psum | solution.py:146
  395.6 30.2 %reduce-scatter.5.cloned.1.call-done = f32[8,2816]{1,0:T(8,128)} async-done(((f32[256,2816]{1,0:T(8,128)}), f32[8,2816]{1,0:T(8,128)}) %reduce-scatter.5.cloned.1.call-update) | async-done | bytes 90128 | tf_op jit(solution)/shard_map/reduce_scatter | solution.py:144
  425.8 2.4 copy.73
  428.2 1.5 fusion.34
  429.8 112.2 %reduce-scatter.7.cloned.1.call-done = f32[176,8]{1,0:T(8,128)} async-done(((f32[2816,8]{1,0:T(8,128)}), f32[176,8]{1,0:T(8,128)}) %reduce-scatter.7.cloned.1.call-update) | async-done | bytes 5648
  542.0 1.6 copy.74
  (62 shorter events, 5.7 us)
Async XLA Ops:
  7.2 51.3 %copy-start.10 = (bf16[1,128,2816]{2,1,0:T(8,128)(2,1)S(1)}, bf16[1,128,2816]{2,1,0:T(8,128)(2,1)}, u32[]{:S(2)}) copy-start(bf16[1,128,2816]{2,1,0:T(8,128)(2,1)} %param.9) | copy-start | bytes 2162692
  7.2 173.0 %all-gather.2.cloned.1.call-start = ((), (), s32[]{:S(2)}) async-start(), calls=%async_computation.2 | async-start | bytes 3829760 | tf_op jit(solution)/shard_map/all_gather | solution.py:86
  58.4 367.3 %reduce-scatter.5.cloned.1.call-start = ((), (), s32[]{:S(2)}) async-start(), calls=%async_computation.3 | async-start | bytes 2973696 | tf_op jit(solution)/shard_map/reduce_scatter | solution.py:144
  58.5 12.2 %collective-permute-start = (bf16[3,2816]{1,0:T(4,128)(2,1)S(1)}, bf16[3,2816]{1,0:T(4,128)(2,1)S(1)}, u32[]{:S(2)}, u32[]{:S(2)}) collective-permute-start(bf16[3,2816]{1,0:T(4,128)(2,1)S(1)} %slice_bitcast_fusion), channel_id=1, source_target_pairs={{0,1},{1,2},{2,3},{3,4},{4,5},{5,6},{6,7},{7,8},{8,9},{9,10},{10,1... | collective-permute-start | bytes 50696 | tf_op jit(solution)/shard_map/ppermute | solution.py:13
  187.7 0.9 copy-start.8
  189.7 3.2 copy-start.4
  203.6 2.8 copy-start.1
  203.6 2.9 copy-start.2
  203.6 2.9 copy-start.9
  206.5 2.8 copy-start.11
  210.6 10.7 %collective-permute-start.5 = (f32[2,2816]{1,0:T(2,128)S(1)}, f32[2,2816]{1,0:T(2,128)S(1)}, u32[]{:S(2)}, u32[]{:S(2)}) collective-permute-start(f32[2,2816]{1,0:T(2,128)S(1)} %get-tuple-element.36), channel_id=1, source_target_pairs={{0,1},{1,2},{2,3},{3,4},{4,5},{5,6},{6,7},{7,8},{8,9},{9,10},{10,1... | collective-permute-start | bytes 67592 | tf_op jit(solution)/shard_map/ppermute | solution.py:13
  215.7 9.6 %collective-permute-start.1 = (f32[2,2816]{1,0:T(2,128)S(1)}, f32[2,2816]{1,0:T(2,128)S(1)}, u32[]{:S(2)}, u32[]{:S(2)}) collective-permute-start(f32[2,2816]{1,0:T(2,128)S(1)} %get-tuple-element.37), channel_id=1, source_target_pairs={{1,0},{2,1},{3,2},{4,3},{5,4},{6,5},{7,6},{8,7},{9,8},{10,9},{11,1... | collective-permute-start | bytes 67592 | tf_op jit(solution)/shard_map/ppermute | solution.py:13
  225.4 15.5 %collective-permute-start.6 = (f32[2,2816]{1,0:T(2,128)S(1)}, f32[2,2816]{1,0:T(2,128)S(1)}, u32[]{:S(2)}, u32[]{:S(2)}) collective-permute-start(f32[2,2816]{1,0:T(2,128)S(1)} %pad_maximum_fusion.6), channel_id=1, source_target_pairs={{0,2},{1,3},{2,4},{3,5},{4,6},{5,7},{6,8},{7,9},{8,10},{9,11},{10,... | collective-permute-start | bytes 67592 | tf_op jit(solution)/shard_map/ppermute | solution.py:13
  232.8 14.4 %collective-permute-start.2 = (f32[2,2816]{1,0:T(2,128)S(1)}, f32[2,2816]{1,0:T(2,128)S(1)}, u32[]{:S(2)}, u32[]{:S(2)}) collective-permute-start(f32[2,2816]{1,0:T(2,128)S(1)} %pad_maximum_fusion.3), channel_id=1, source_target_pairs={{2,0},{3,1},{4,2},{5,3},{6,4},{7,5},{8,6},{9,7},{10,8},{11,9},{12,... | collective-permute-start | bytes 67592 | tf_op jit(solution)/shard_map/ppermute | solution.py:13
  241.0 9.0 %collective-permute-start.7 = (f32[2,2816]{1,0:T(2,128)S(1)}, f32[2,2816]{1,0:T(2,128)S(1)}, u32[]{:S(2)}, u32[]{:S(2)}) collective-permute-start(f32[2,2816]{1,0:T(2,128)S(1)} %pad_maximum_fusion.7), channel_id=1, source_target_pairs={{0,4},{1,5},{2,6},{3,7},{4,8},{5,9},{6,10},{7,11},{8,12},{9,13},{1... | collective-permute-start | bytes 67592 | tf_op jit(solution)/shard_map/ppermute | solution.py:13
  247.3 4.2 collective-permute-start.3
  250.1 7.4 %collective-permute-start.8 = (f32[2,2816]{1,0:T(2,128)S(1)}, f32[2,2816]{1,0:T(2,128)S(1)}, u32[]{:S(2)}, u32[]{:S(2)}) collective-permute-start(f32[2,2816]{1,0:T(2,128)S(1)} %pad_maximum_fusion.8), channel_id=1, source_target_pairs={{0,8},{1,9},{2,10},{3,11},{4,12},{5,13},{6,14},{7,15},{16,24},{17,... | collective-permute-start | bytes 67592 | tf_op jit(solution)/shard_map/ppermute | solution.py:13
  251.6 7.5 %collective-permute-start.4 = (f32[2,2816]{1,0:T(2,128)S(1)}, f32[2,2816]{1,0:T(2,128)S(1)}, u32[]{:S(2)}, u32[]{:S(2)}) collective-permute-start(f32[2,2816]{1,0:T(2,128)S(1)} %pad_maximum_fusion.5), channel_id=1, source_target_pairs={{8,0},{9,1},{10,2},{11,3},{12,4},{13,5},{14,6},{15,7},{24,16},{25,... | collective-permute-start | bytes 67592 | tf_op jit(solution)/shard_map/ppermute | solution.py:13
  265.1 1.5 copy-start.5
  266.6 2.2 copy-start.6
  272.1 1.4 copy-start
  272.2 269.8 %reduce-scatter.7.cloned.1.call-start = ((), (), s32[]{:S(2)}) async-start(), calls=%async_computation.4 | async-start | bytes 1531904
  276.3 3.0 copy-start.7
  282.2 1.6 copy-start.3
  286.4 141.8 %collective-permute-start.9 = (f32[3,2816]{1,0:T(4,128)S(1)}, f32[3,2816]{1,0:T(4,128)S(1)}, u32[]{:S(2)}, u32[]{:S(2)}) collective-permute-start(f32[3,2816]{1,0:T(4,128)S(1)} %slice.199), channel_id=1, source_target_pairs={{1,0},{2,1},{3,2},{4,3},{5,4},{6,5},{7,6},{8,7},{9,8},{10,9},{11,1... | collective-permute-start | bytes 101384 | tf_op jit(solution)/shard_map/ppermute | solution.py:13
Sparse Core Ops, SparseCore 0:
  58.6 121.5 all-gather.1
  272.3 153.4 reduce-scatter.4
  429.9 112.0 reduce-scatter.6

commit v2 on v1

--- a/solution.py
+++ b/solution.py
@@ -66,6 +66,21 @@
     return fwd_excl[1], bwd_excl[1]
 
 
+def summed_apart(parts, shared, axis):
+    count, size = parts.shape
+    stacked = jnp.concatenate(
+        [parts, jnp.broadcast_to(shared[None], (count, shared.shape[0]))], 1
+    )
+    sublanes = 8
+    total = stacked.shape[1]
+    tile = sublanes * 256
+    padded = -(-total // tile) * tile
+    stacked = jnp.pad(stacked, ((0, 0), (0, padded - total)))
+    stacked = stacked.reshape(count * sublanes, padded // sublanes)
+    mine = lax.psum_scatter(stacked, axis, scatter_dimension=0, tiled=True).reshape(-1)
+    return mine[:size], mine[size:total]
+
+
 def on_device(
     branch_in, cotangent, weight_a, weight_x, conv_weight, conv_bias, bias_a, bias_x, rate
 ):
@@ -79,11 +94,12 @@
     packed = jnp.concatenate(
         [conv_weight, conv_bias[None], bias_a[None], bias_x[None], rate[None]], 0
     )
-    param_rows = packed.shape[0]
-    both = lax.all_gather(jnp.stack([weight_a, weight_x]), "dp", axis=1, tiled=True)
-    head_width = both.shape[1]
+    both = lax.all_gather(jnp.concatenate([weight_a, weight_x], 0), "dp", axis=0, tiled=True)
+    both = both.reshape(dp_size, 2, rows, cols).transpose(1, 0, 2, 3)
+    head_width = dp_size * rows
     joined = jnp.concatenate([both.reshape(2 * head_width, cols), packed], 0)
-    joined = lax.all_gather(joined, "ctx", axis=1, tiled=True)
+    joined = lax.all_gather(joined, "ctx", axis=0, tiled=True)
+    joined = joined.reshape(ctx_size, -1, cols).transpose(1, 0, 2).reshape(-1, ctx_size * cols)
     full_a = joined[:head_width]
     full_x = joined[head_width : 2 * head_width]
     params = joined[2 * head_width :]
@@ -141,9 +157,12 @@
         start = taps - 1 - tap
         grad_in = grad_in + taps_f[tap] * dpad[start : start + length]
     local_wgrad = grad_heads(conv_b, d_recur, head_width)
-    row_part = lax.psum_scatter(local_wgrad, "dp", scatter_dimension=0, tiled=True)
-    wgrad = lax.psum_scatter(row_part, "ctx", scatter_dimension=1, tiled=True)
-    rgrad = lax.psum(jnp.sum(d_log * (-8.0 * recur_gate), axis=0), ("dp", "ctx"))
+    local_rgrad = jnp.sum(d_log * (-8.0 * recur_gate), axis=0)
+    by_channel = local_wgrad.reshape(head_width, ctx_size, cols).transpose(1, 0, 2)
+    channel_sum, rgrad = summed_apart(by_channel.reshape(ctx_size, -1), local_rgrad, "ctx")
+    by_row = channel_sum.reshape(dp_size, rows * cols)
+    row_sum, rgrad = summed_apart(by_row, rgrad, "dp")
+    wgrad = row_sum.reshape(rows, cols)
     return (grad_in.astype(jnp.bfloat16)[None], wgrad, rgrad)
 
 

time: 553 us -> 592 us (1.071)
  waiting for transfers between devices: 265 us -> 388 us
  blocking collectives: 148 us -> 45.6 us
  local copies, waits for them, and re-layouts: 31.8 us -> 46.7 us
    reduce_scatter x1 -> x2, waiting for transfers between devices: 30.2 us -> 262 us  [summed_apart(): lax.psum_scatter(stacked, axis, scatter_dimension=0, tiled=True).reshape(-1)]
    unnamed x4 -> x3, waiting for transfers between devices: 112 us -> 0.05 us
    psum x1 -> x0, blocking collectives: 102 us -> none  [on_device(): lax.psum(jnp.sum(d_log * (-8.0 * recur_gate), axis=0), ('dp', 'ctx'))]
    reshape x2 -> x7, local copies, waits for them, and re-layouts: 3.5 us -> 12.9 us  [the longest x1 5.8 us: on_device(): by_channel.reshape(ctx_size, -1)]
  transfers between devices with their start and end apart: 13 -> 13, of which waited for: 8 -> 9; matrix products, arithmetic and copies ran while one was open for 3% -> 2% of each run, Pallas kernels for 0% -> 0%
where the time goes in v2:
time: 592 us; the launch traced here: 590 us
  waiting for transfers between devices  388 us (66%)
  starting transfers between devices  53.4 us (9%)
  local copies, waits for them, and re-layouts  46.7 us (8%)
  blocking collectives  45.6 us (8%)
  other arithmetic  23.1 us (4%)
  matrix products  19.6 us (3%)
  between operations  14.2 us (2%)
    reduce_scatter x2, waiting for transfers between devices, summed_apart(): lax.psum_scatter(stacked, axis, scatter_dimension=0, tiled=True).reshape(-1)  262 us
    all_gather x1, waiting for transfers between devices, on_device(): joined = lax.all_gather(joined, 'ctx', axis=0, tiled=True)  109 us
    ppermute x10, starting transfers between devices, passed_along(): return lax.ppermute(array, axis, pairs)  53 us
    all_gather x1, blocking collectives, on_device(): lax.all_gather(jnp.concatenate([weight_a, weight_x], 0), 'dp', axis=0, ti...  45.6 us
    ppermute x10, waiting for transfers between devices, passed_along(): return lax.ppermute(array, axis, pairs)  16.7 us
  transfers between devices with their start and end apart: 13, of which 9 were waited for; matrix products, arithmetic and copies ran while one was open for 2% of the time, Pallas kernels for 0%

profile of v2, /device:TPU:6, one launch (start us, length us, event | category | flops | bytes accessed | tf_op | source)
XLA Modules:
  0.0 590.3 jit_solution(10837949532559104495)
XLA Ops:
  10.6 45.6 %all_gather.6 = bf16[512,176]{1,0:T(8,128)(2,1)S(1)} all-gather(bf16[16,176]{1,0:T(8,128)(2,1)S(1)} %pad_maximum_fusion.11), channel_id=1, replica_groups=mesh['dp'=32,'ctx'=16] {'dp'}, dimensions={0}, use_global_device_ids=true | all-gather | bytes 185856 | tf_op jit(solution)/shard_map/all_gather | solution.py:97
  58.0 9.1 %collective-permute-start = (bf16[3,2816]{1,0:T(4,128)(2,1)S(1)}, bf16[3,2816]{1,0:T(4,128)(2,1)S(1)}, u32[]{:S(2)}, u32[]{:S(2)}) collective-permute-start(bf16[3,2816]{1,0:T(4,128)(2,1)S(1)} %slice_bitcast_fusion), channel_id=1, source_target_pairs={{0,1},{1,2},{2,3},{3,4},{4,5},{5,6},{6,7},{7,8},{8,9},{9,10},{10,1... | collective-permute-start | bytes 50696 | tf_op jit(solution)/shard_map/ppermute | solution.py:13
  67.1 3.1 collective-permute-done
  70.4 109.3 %all-gather.3.cloned.1.call-done = bf16[16,520,176]{1,2,0:T(8,128)(2,1)} async-done(((bf16[1,520,176]{1,2,0:T(8,128)(2,1)}), bf16[16,520,176]{1,2,0:T(8,128)(2,1)}) %all-gather.3.cloned.1.call-update) | async-done | bytes 2928656 | tf_op jit(solution)/shard_map/all_gather | solution.py:101
  179.7 1.2 slice_convert_fusion
  180.9 3.1 fusion.45
  184.0 7.0 %slice_reduce_fusion = (f32[16,176]{1,0:T(8,128)S(1)}, f32[16,176]{1,0:T(8,128)S(1)}, f32[16,176]{1,0:T(8,128)S(1)}, f32[16,176]{1,0:T(8,128)S(1)}, f32[16,176]{...) fusion(f32[8,16,176]{0,2,1:T(8,128)S(1)} %slice_convert_fusion), kind=kLoop, calls=%fused_computation.29 | loop fusion | flops 2816 | bytes 180224 | tf_op jit(solution)/shard_map/slice | solution.py:110
  191.7 1.5 fusion.19
  193.2 2.3 copy.46
  195.5 2.8 fusion.48
  198.3 2.9 copy.50
  201.2 3.2 fusion.47
  204.5 2.9 copy.48
  207.4 2.8 fusion.46
  210.3 2.9 convolution_multiply_fusion
  213.2 1.1 fusion.24
  214.4 5.1 collective-permute-start.5
  219.5 5.6 collective-permute-start.1
  225.1 4.0 collective-permute-done.1
  229.2 7.3 %collective-permute-start.6 = (f32[2,2816]{1,0:T(2,128)S(1)}, f32[2,2816]{1,0:T(2,128)S(1)}, u32[]{:S(2)}, u32[]{:S(2)}) collective-permute-start(f32[2,2816]{1,0:T(2,128)S(1)} %pad_maximum_fusion.8), channel_id=1, source_target_pairs={{0,2},{1,3},{2,4},{3,5},{4,6},{5,7},{6,8},{7,9},{8,10},{9,11},{10,... | collective-permute-start | bytes 67592 | tf_op jit(solution)/shard_map/ppermute | solution.py:13
  236.6 8.1 %collective-permute-start.2 = (f32[2,2816]{1,0:T(2,128)S(1)}, f32[2,2816]{1,0:T(2,128)S(1)}, u32[]{:S(2)}, u32[]{:S(2)}) collective-permute-start(f32[2,2816]{1,0:T(2,128)S(1)} %pad_maximum_fusion.5), channel_id=1, source_target_pairs={{2,0},{3,1},{4,2},{5,3},{6,4},{7,5},{8,6},{9,7},{10,8},{11,9},{12,... | collective-permute-start | bytes 67592 | tf_op jit(solution)/shard_map/ppermute | solution.py:13
  244.8 1.3 collective-permute-start.7
  246.1 4.9 collective-permute-done.2
  251.0 2.8 collective-permute-start.3
  253.9 1.3 collective-permute-start.8
  255.3 6.0 %collective-permute-start.4 = (f32[2,2816]{1,0:T(2,128)S(1)}, f32[2,2816]{1,0:T(2,128)S(1)}, u32[]{:S(2)}, u32[]{:S(2)}) collective-permute-start(f32[2,2816]{1,0:T(2,128)S(1)} %pad_maximum_fusion.7), channel_id=1, source_target_pairs={{8,0},{9,1},{10,2},{11,3},{12,4},{13,5},{14,6},{15,7},{24,16},{25,... | collective-permute-start | bytes 67592 | tf_op jit(solution)/shard_map/ppermute | solution.py:13
  261.6 1.2 collective-permute-done.4
  262.9 4.6 multiply_reduce_fusion
  267.5 1.3 multiply_convert_fusion
  268.8 1.5 copy.51
  270.3 2.1 fusion.51
  272.5 4.8 copy.60
  277.3 5.8 reshape.115
  283.1 2.1 pad_maximum_fusion
  285.2 1.9 pad.8
  287.1 3.4 reshape.116
  291.8 2.8 fusion.49
  294.7 3.0 copy.54
  297.7 1.1 copy.55
  298.8 1.7 fusion.50
  300.5 1.5 copy.58
  302.1 129.5 %reduce-scatter.3.cloned.1.call-done = f32[8,6144]{1,0:T(8,128)} async-done(((f32[128,6144]{1,0:T(8,128)}), f32[8,6144]{1,0:T(8,128)}) %reduce-scatter.3.cloned.1.call-update) | async-done | bytes 196624 | tf_op jit(solution)/shard_map/reduce_scatter | solution.py:80
  433.6 2.3 reshape.119
  435.9 2.2 add_add_fusion
  438.2 6.5 %collective-permute-start.9 = (f32[3,2816]{1,0:T(4,128)S(1)}, f32[3,2816]{1,0:T(4,128)S(1)}, u32[]{:S(2)}, u32[]{:S(2)}) collective-permute-start(f32[3,2816]{1,0:T(4,128)S(1)} %slice.226), channel_id=1, source_target_pairs={{1,0},{2,1},{3,2},{4,3},{5,4},{6,5},{7,6},{8,7},{9,8},{10,9},{11,1... | collective-permute-start | bytes 101384 | tf_op jit(solution)/shard_map/ppermute | solution.py:13
  444.7 3.3 collective-permute-done.9
  448.0 1.5 fusion.34
  449.5 132.2 %reduce-scatter.5.cloned.1.call-done = f32[8,768]{1,0:T(8,128)} async-done(((f32[256,768]{1,0:T(8,128)}), f32[8,768]{1,0:T(8,128)}) %reduce-scatter.5.cloned.1.call-update) | async-done | bytes 24592 | tf_op jit(solution)/shard_map/reduce_scatter | solution.py:80
  (82 shorter events, 12.2 us)
Async XLA Ops:
  7.2 50.8 %copy-start.9 = (bf16[1,128,2816]{2,1,0:T(8,128)(2,1)S(1)}, bf16[1,128,2816]{2,1,0:T(8,128)(2,1)}, u32[]{:S(2)}) copy-start(bf16[1,128,2816]{2,1,0:T(8,128)(2,1)} %param.9) | copy-start | bytes 2162692
  7.2 172.5 %all-gather.3.cloned.1.call-start = ((), (), s32[]{:S(2)}) async-start(), calls=%async_computation.4 | async-start | bytes 3829760 | tf_op jit(solution)/shard_map/all_gather | solution.py:101
  57.9 373.6 %reduce-scatter.3.cloned.1.call-start = ((), (), s32[]{:S(2)}) async-start(), calls=%async_computation.2 | async-start | bytes 3342336 | tf_op jit(solution)/shard_map/reduce_scatter | solution.py:80
  58.0 12.2 %collective-permute-start = (bf16[3,2816]{1,0:T(4,128)(2,1)S(1)}, bf16[3,2816]{1,0:T(4,128)(2,1)S(1)}, u32[]{:S(2)}, u32[]{:S(2)}) collective-permute-start(bf16[3,2816]{1,0:T(4,128)(2,1)S(1)} %slice_bitcast_fusion), channel_id=1, source_target_pairs={{0,1},{1,2},{2,3},{3,4},{4,5},{5,6},{6,7},{7,8},{8,9},{9,10},{10,1... | collective-permute-start | bytes 50696 | tf_op jit(solution)/shard_map/ppermute | solution.py:13
  207.4 2.8 copy-start.1
  207.4 2.9 copy-start.2
  207.4 2.9 copy-start.8
  210.2 3.0 copy-start.10
  214.4 10.7 %collective-permute-start.5 = (f32[2,2816]{1,0:T(2,128)S(1)}, f32[2,2816]{1,0:T(2,128)S(1)}, u32[]{:S(2)}, u32[]{:S(2)}) collective-permute-start(f32[2,2816]{1,0:T(2,128)S(1)} %get-tuple-element.36), channel_id=1, source_target_pairs={{0,1},{1,2},{2,3},{3,4},{4,5},{5,6},{6,7},{7,8},{8,9},{9,10},{10,1... | collective-permute-start | bytes 67592 | tf_op jit(solution)/shard_map/ppermute | solution.py:13
  219.5 9.6 %collective-permute-start.1 = (f32[2,2816]{1,0:T(2,128)S(1)}, f32[2,2816]{1,0:T(2,128)S(1)}, u32[]{:S(2)}, u32[]{:S(2)}) collective-permute-start(f32[2,2816]{1,0:T(2,128)S(1)} %get-tuple-element.37), channel_id=1, source_target_pairs={{1,0},{2,1},{3,2},{4,3},{5,4},{6,5},{7,6},{8,7},{9,8},{10,9},{11,1... | collective-permute-start | bytes 67592 | tf_op jit(solution)/shard_map/ppermute | solution.py:13
  229.2 15.5 %collective-permute-start.6 = (f32[2,2816]{1,0:T(2,128)S(1)}, f32[2,2816]{1,0:T(2,128)S(1)}, u32[]{:S(2)}, u32[]{:S(2)}) collective-permute-start(f32[2,2816]{1,0:T(2,128)S(1)} %pad_maximum_fusion.8), channel_id=1, source_target_pairs={{0,2},{1,3},{2,4},{3,5},{4,6},{5,7},{6,8},{7,9},{8,10},{9,11},{10,... | collective-permute-start | bytes 67592 | tf_op jit(solution)/shard_map/ppermute | solution.py:13
  236.6 14.4 %collective-permute-start.2 = (f32[2,2816]{1,0:T(2,128)S(1)}, f32[2,2816]{1,0:T(2,128)S(1)}, u32[]{:S(2)}, u32[]{:S(2)}) collective-permute-start(f32[2,2816]{1,0:T(2,128)S(1)} %pad_maximum_fusion.5), channel_id=1, source_target_pairs={{2,0},{3,1},{4,2},{5,3},{6,4},{7,5},{8,6},{9,7},{10,8},{11,9},{12,... | collective-permute-start | bytes 67592 | tf_op jit(solution)/shard_map/ppermute | solution.py:13
  244.8 9.0 %collective-permute-start.7 = (f32[2,2816]{1,0:T(2,128)S(1)}, f32[2,2816]{1,0:T(2,128)S(1)}, u32[]{:S(2)}, u32[]{:S(2)}) collective-permute-start(f32[2,2816]{1,0:T(2,128)S(1)} %pad_maximum_fusion.9), channel_id=1, source_target_pairs={{0,4},{1,5},{2,6},{3,7},{4,8},{5,9},{6,10},{7,11},{8,12},{9,13},{1... | collective-permute-start | bytes 67592 | tf_op jit(solution)/shard_map/ppermute | solution.py:13
  251.0 4.2 collective-permute-start.3
  253.9 7.4 %collective-permute-start.8 = (f32[2,2816]{1,0:T(2,128)S(1)}, f32[2,2816]{1,0:T(2,128)S(1)}, u32[]{:S(2)}, u32[]{:S(2)}) collective-permute-start(f32[2,2816]{1,0:T(2,128)S(1)} %pad_maximum_fusion.10), channel_id=1, source_target_pairs={{0,8},{1,9},{2,10},{3,11},{4,12},{5,13},{6,14},{7,15},{16,24},{17,... | collective-permute-start | bytes 67592 | tf_op jit(solution)/shard_map/ppermute | solution.py:13
  255.3 7.5 %collective-permute-start.4 = (f32[2,2816]{1,0:T(2,128)S(1)}, f32[2,2816]{1,0:T(2,128)S(1)}, u32[]{:S(2)}, u32[]{:S(2)}) collective-permute-start(f32[2,2816]{1,0:T(2,128)S(1)} %pad_maximum_fusion.7), channel_id=1, source_target_pairs={{8,0},{9,1},{10,2},{11,3},{12,4},{13,5},{14,6},{15,7},{24,16},{25,... | collective-permute-start | bytes 67592 | tf_op jit(solution)/shard_map/ppermute | solution.py:13
  268.8 1.5 copy-start.4
  270.3 2.2 copy-start.5
  290.5 1.4 copy-start
  290.5 291.2 %reduce-scatter.5.cloned.1.call-start = ((), (), s32[]{:S(2)}) async-start(), calls=%async_computation.3 | async-start | bytes 811008 | tf_op jit(solution)/shard_map/reduce_scatter | solution.py:80
  294.7 3.0 copy-start.7
  432.7 3.2 copy-start.6
  433.6 2.3 copy-start.3
  438.2 9.9 %collective-permute-start.9 = (f32[3,2816]{1,0:T(4,128)S(1)}, f32[3,2816]{1,0:T(4,128)S(1)}, u32[]{:S(2)}, u32[]{:S(2)}) collective-permute-start(f32[3,2816]{1,0:T(4,128)S(1)} %slice.226), channel_id=1, source_target_pairs={{1,0},{2,1},{3,2},{4,3},{5,4},{6,5},{7,6},{8,7},{9,8},{10,9},{11,1... | collective-permute-start | bytes 101384 | tf_op jit(solution)/shard_map/ppermute | solution.py:13
Sparse Core Ops, SparseCore 0:
  58.1 121.5 all-gather.2
  290.6 140.9 reduce-scatter.2
  436.0 145.6 reduce-scatter.4

commit v3 on v2

--- a/solution.py
+++ b/solution.py
@@ -66,20 +66,48 @@
     return fwd_excl[1], bwd_excl[1]
 
 
+def exchanged(array, axis, stride):
+    length = lax.axis_size(axis)
+    return lax.ppermute(array, axis, [(i, i ^ stride) for i in range(length)])
+
+
+def gathered_by_doubling(piece, axis):
+    length = lax.axis_size(axis)
+    me = lax.axis_index(axis)
+    held = piece[None]
+    stride = 1
+    while stride < length:
+        got = exchanged(held, axis, stride)
+        upper = (me // stride) % 2 == 1
+        low = jnp.where(upper, got, held)
+        high = jnp.where(upper, held, got)
+        held = jnp.concatenate([low, high], 0)
+        stride *= 2
+    return held
+
+
+def summed_by_halving(blocks, axis):
+    length = lax.axis_size(axis)
+    me = lax.axis_index(axis)
+    held = blocks
+    stride = length // 2
+    while stride >= 1:
+        halves = held.reshape((2, held.shape[0] // 2) + held.shape[1:])
+        upper = ((me // stride) % 2).astype(jnp.int32)
+        keep = lax.dynamic_index_in_dim(halves, upper, 0, keepdims=False)
+        give = lax.dynamic_index_in_dim(halves, 1 - upper, 0, keepdims=False)
+        held = keep + exchanged(give, axis, stride)
+        stride //= 2
+    return held[0]
+
+
 def summed_apart(parts, shared, axis):
     count, size = parts.shape
     stacked = jnp.concatenate(
         [parts, jnp.broadcast_to(shared[None], (count, shared.shape[0]))], 1
     )
-    sublanes = 8
-    total = stacked.shape[1]
-    tile = sublanes * 256
-    padded = -(-total // tile) * tile
-    stacked = jnp.pad(stacked, ((0, 0), (0, padded - total)))
-    stacked = stacked.reshape(count * sublanes, padded // sublanes)
-    mine = lax.psum_scatter(stacked, axis, scatter_dimension=0, tiled=True).reshape(-1)
-    return mine[:size], mine[size:total]
-
+    mine = summed_by_halving(stacked, axis)
+    return mine[:size], mine[size:]
 
 def on_device(
     branch_in, cotangent, weight_a, weight_x, conv_weight, conv_bias, bias_a, bias_x, rate
@@ -98,8 +126,8 @@
     both = both.reshape(dp_size, 2, rows, cols).transpose(1, 0, 2, 3)
     head_width = dp_size * rows
     joined = jnp.concatenate([both.reshape(2 * head_width, cols), packed], 0)
-    joined = lax.all_gather(joined, "ctx", axis=0, tiled=True)
-    joined = joined.reshape(ctx_size, -1, cols).transpose(1, 0, 2).reshape(-1, ctx_size * cols)
+    joined = gathered_by_doubling(joined, "ctx")
+    joined = joined.transpose(1, 0, 2).reshape(-1, ctx_size * cols)
     full_a = joined[:head_width]
     full_x = joined[head_width : 2 * head_width]
     params = joined[2 * head_width :]

time: 592 us -> 496 us (0.84)
  waiting for transfers between devices: 388 us -> 204 us
  starting transfers between devices: 53.4 us -> 122 us
  local copies, waits for them, and re-layouts: 46.7 us -> 65.2 us
  between operations: 14.2 us -> 1.82 us
  other arithmetic: 23.1 us -> 33 us
    reduce_scatter x2 -> x0, waiting for transfers between devices: 262 us -> none  [summed_apart(): lax.psum_scatter(stacked, axis, scatter_dimension=0, tiled=True).reshape(-1)]
    ppermute x0 -> x13, waiting for transfers between devices: none -> 183 us  [exchanged(): return lax.ppermute(array, axis, [(i, i ^ stride) for i in range(length)])]
    all_gather x1 -> x0, waiting for transfers between devices: 109 us -> none  [on_device(): joined = lax.all_gather(joined, 'ctx', axis=0, tiled=True)]
    ppermute x0 -> x13, starting transfers between devices: none -> 80.8 us  [exchanged(): return lax.ppermute(array, axis, [(i, i ^ stride) for i in range(length)])]
    ppermute x10, starting transfers between devices: 53 us -> 41.6 us  [passed_along(): return lax.ppermute(array, axis, pairs)]
    reshape x5 -> x4, local copies, waits for them, and re-layouts: 12.2 us -> 3.4 us  [summed_by_halving(): halves = held.reshape((2, held.shape[0] // 2) + held.shape[1:])]
    slice x1, other arithmetic: 7.01 us -> 0.36 us  [on_device(): xbias = params[taps + 2]]
    concatenate x2 -> x4, local copies, waits for them, and re-layouts: 0.02 us -> 6.56 us  [summed_apart(): jnp.concatenate([parts, jnp.broadcast_to(shared[None], (count, shared.sha...]
  transfers between devices with their start and end apart: 13 -> 23, of which waited for: 9 -> 15; matrix products, arithmetic and copies ran while one was open for 2% -> 4% of each run, Pallas kernels for 0% -> 0%
where the time goes in v3:
time: 496 us; the launch traced here: 494 us
  waiting for transfers between devices  204 us (41%)
  starting transfers between devices  122 us (25%)
  local copies, waits for them, and re-layouts  65.2 us (13%)
  blocking collectives  45.6 us (9%)
  other arithmetic  33 us (7%)
  matrix products  22 us (4%)
    ppermute x13, waiting for transfers between devices, exchanged(): return lax.ppermute(array, axis, [(i, i ^ stride) for i in range(length)])  183 us
    ppermute x13, starting transfers between devices, exchanged(): return lax.ppermute(array, axis, [(i, i ^ stride) for i in range(length)])  80.8 us
    all_gather x1, blocking collectives, on_device(): lax.all_gather(jnp.concatenate([weight_a, weight_x], 0), 'dp', axis=0, ti...  45.6 us
    ppermute x10, starting transfers between devices, passed_along(): return lax.ppermute(array, axis, pairs)  41.6 us
    ppermute x10, waiting for transfers between devices, passed_along(): return lax.ppermute(array, axis, pairs)  21.5 us
  transfers between devices with their start and end apart: 23, of which 15 were waited for; matrix products, arithmetic and copies ran while one was open for 4% of the time, Pallas kernels for 0%

profile of v3, /device:TPU:6, one launch (start us, length us, event | category | flops | bytes accessed | tf_op | source)
XLA Modules:
  0.0 494.3 jit_solution(14537777870435538084)
XLA Ops:
  1.3 45.6 %all_gather.3 = bf16[512,176]{1,0:T(8,128)(2,1)S(1)} all-gather(bf16[16,176]{1,0:T(8,128)(2,1)S(1)} %pad_maximum_fusion.14), channel_id=1, replica_groups=mesh['dp'=32,'ctx'=16] {'dp'}, dimensions={0}, use_global_device_ids=true | all-gather | bytes 185856 | tf_op jit(solution)/shard_map/all_gather | solution.py:125
  50.4 9.1 %collective-permute-start = (bf16[1,520,176]{2,1,0:T(8,128)(2,1)S(1)}, bf16[1,520,176]{2,1,0:T(8,128)(2,1)S(1)}, u32[]{:S(2)}, u32[]{:S(2)}) collective-permute-start(bf16[1,520,176]{2,1,0:T(8,128)(2,1)S(1)} %bitcast.99), channel_id=1, source_target_pairs={{0,1},{1,0},{2,3},{3,2},{4,5},{5,4},{6,7},{7,6},{8,9},{9,8},{10,11... | collective-permute-start | bytes 549128 | tf_op jit(solution)/shard_map/ppermute | solution.py:71
  59.5 16.4 %collective-permute-done = bf16[1,520,176]{2,1,0:T(8,128)(2,1)S(1)} collective-permute-done((bf16[1,520,176]{2,1,0:T(8,128)(2,1)S(1)}, bf16[1,520,176]{2,1,0:T(8,128)(2,1)S(1)}, u32[]{:S(2)}, u32[]{:S(2)}) %collective-permute-start) | collective-permute-done | bytes 183072 | tf_op jit(solution)/shard_map/ppermute | solution.py:71
  76.4 23.0 %collective-permute-start.1 = (bf16[2,520,176]{1,2,0:T(8,128)(2,1)S(1)}, bf16[2,520,176]{1,2,0:T(8,128)(2,1)S(1)}, u32[]{:S(2)}, u32[]{:S(2)}) collective-permute-start(bf16[2,520,176]{1,2,0:T(8,128)(2,1)S(1)} %copy.45), channel_id=1, source_target_pairs={{0,2},{1,3},{2,0},{3,1},{4,6},{5,7},{6,4},{7,5},{8,10},{9,11},{10,... | collective-permute-start | bytes 1098248 | tf_op jit(solution)/shard_map/ppermute | solution.py:71
  99.4 30.4 %collective-permute-done.1 = bf16[2,520,176]{1,2,0:T(8,128)(2,1)S(1)} collective-permute-done((bf16[2,520,176]{1,2,0:T(8,128)(2,1)S(1)}, bf16[2,520,176]{1,2,0:T(8,128)(2,1)S(1)}, u32[]{:S(2)}, u32[]{:S(2)}) %collective-permute-start.1) | collective-permute-done | bytes 366112 | tf_op jit(solution)/shard_map/ppermute | solution.py:71
  131.1 2.7 collective-permute-start.2
  133.8 21.0 %collective-permute-done.2 = bf16[4,520,176]{1,2,0:T(8,128)(2,1)S(1)} collective-permute-done((bf16[4,520,176]{1,2,0:T(8,128)(2,1)S(1)}, bf16[4,520,176]{1,2,0:T(8,128)(2,1)S(1)}, u32[]{:S(2)}, u32[]{:S(2)}) %collective-permute-start.2) | collective-permute-done | bytes 732192 | tf_op jit(solution)/shard_map/ppermute | solution.py:71
  160.4 4.0 copy.51
  164.4 3.3 collective-permute-start.3
  170.7 8.5 %collective-permute-done.4 = bf16[3,2816]{1,0:T(4,128)(2,1)S(1)} collective-permute-done((bf16[3,2816]{1,0:T(4,128)(2,1)S(1)}, bf16[3,2816]{1,0:T(4,128)(2,1)S(1)}, u32[]{:S(2)}, u32[]{:S(2)}) %collective-permute-start.4) | collective-permute-done | bytes 16928 | tf_op jit(solution)/shard_map/ppermute | solution.py:13
  180.4 28.1 %collective-permute-done.3 = bf16[8,520,176]{1,2,0:T(8,128)(2,1)} collective-permute-done((bf16[8,520,176]{1,2,0:T(8,128)(2,1)}, bf16[8,520,176]{1,2,0:T(8,128)(2,1)}, u32[]{:S(2)}, u32[]{:S(2)}) %collective-permute-start.3) | collective-permute-done | bytes 1464352 | tf_op jit(solution)/shard_map/ppermute | solution.py:71
  208.5 3.9 copy.52
  212.4 2.4 broadcast_select_fusion.1
  215.5 2.5 fusion.46
  220.6 3.0 copy.54
  223.5 3.3 fusion.48
  228.8 2.4 fusion.47
  233.5 3.0 copy.58
  236.4 2.8 fusion.49
  239.2 3.0 copy.60
  242.2 5.6 %convolution_multiply_fusion = f32[128,2816]{1,0:T(8,128)S(1)} fusion(bf16[128,2816]{1,0:T(8,128)(2,1)} %copy-done.17, f32[128,2816]{1,0:T(8,128)} %copy-done.15, f32[2816]{0:T(1024)S(1)} %mul.312, f32[128,2816]{1,0:T(8,128)} %copy.60, f32[2816]{0:T(1024)S(1)} %add.281, f32[128,2816]{1,0:T(8,128)} %copy-done.2, f32[2816]{0:T(1024)S(1)} %add.270), kind=kOutput, calls=%fused_computation.1 | convolution fusion | flops 560152576 | bytes 6521856 | tf_op jit(solution)/shard_map/dot_general | solution.py:163
  251.9 7.8 %collective-permute-start.9 = (f32[2,2816]{1,0:T(2,128)S(1)}, f32[2,2816]{1,0:T(2,128)S(1)}, u32[]{:S(2)}, u32[]{:S(2)}) collective-permute-start(f32[2,2816]{1,0:T(2,128)S(1)} %get-tuple-element.44), channel_id=1, source_target_pairs={{0,1},{1,2},{2,3},{3,4},{4,5},{5,6},{6,7},{7,8},{8,9},{9,10},{10,1... | collective-permute-start | bytes 67592 | tf_op jit(solution)/shard_map/ppermute | solution.py:13
  259.7 2.6 collective-permute-done.9
  263.4 6.4 %collective-permute-start.10 = (f32[2,2816]{1,0:T(2,128)S(1)}, f32[2,2816]{1,0:T(2,128)S(1)}, u32[]{:S(2)}, u32[]{:S(2)}) collective-permute-start(f32[2,2816]{1,0:T(2,128)S(1)} %pad_maximum_fusion.11), channel_id=1, source_target_pairs={{0,2},{1,3},{2,4},{3,5},{4,6},{5,7},{6,8},{7,9},{8,10},{9,11},{10,... | collective-permute-start | bytes 67592 | tf_op jit(solution)/shard_map/ppermute | solution.py:13
  269.9 9.1 %collective-permute-start.6 = (f32[2,2816]{1,0:T(2,128)S(1)}, f32[2,2816]{1,0:T(2,128)S(1)}, u32[]{:S(2)}, u32[]{:S(2)}) collective-permute-start(f32[2,2816]{1,0:T(2,128)S(1)} %pad_maximum_fusion.8), channel_id=1, source_target_pairs={{2,0},{3,1},{4,2},{5,3},{6,4},{7,5},{8,6},{9,7},{10,8},{11,9},{12,... | collective-permute-start | bytes 67592 | tf_op jit(solution)/shard_map/ppermute | solution.py:13
  280.3 4.0 collective-permute-done.6
  284.4 3.6 collective-permute-start.7
  289.5 6.2 %collective-permute-start.8 = (f32[2,2816]{1,0:T(2,128)S(1)}, f32[2,2816]{1,0:T(2,128)S(1)}, u32[]{:S(2)}, u32[]{:S(2)}) collective-permute-start(f32[2,2816]{1,0:T(2,128)S(1)} %pad_maximum_fusion.10), channel_id=1, source_target_pairs={{8,0},{9,1},{10,2},{11,3},{12,4},{13,5},{14,6},{15,7},{24,16},{25,... | collective-permute-start | bytes 67592 | tf_op jit(solution)/shard_map/ppermute | solution.py:13
  298.9 5.7 %multiply_reduce_fusion = (f32[2816]{0:T(1024)S(1)}, f32[128,2816]{1,0:T(8,128)S(1)}, bf16[128,2816]{1,0:T(8,128)(2,1)}, f32[128,2816]{1,0:T(8,128)}) fusion(f32[128,2816]{1,0:T(8,128)S(1)} %copy-done.3, f32[2816]{0:T(1024)S(1)} %add.270, f32[128,2816]{1,0:T(8,128)S(1)} %copy-done.4, f32[2816]{0:T(1024)S(1)} %add.281, f32[2816]{0:T(1024)S(1)} %mul.312, ...), kind=kLoop, calls=%fused_computation.48 | loop fusion | flops 17659136 | bytes 16704512 | tf_op jit(solution)/shard_map/reduce_sum | solution.py:188
  309.6 4.8 copy.70
  314.4 5.8 %concatenate.48 = f32[2,8,45056]{2,1,0:T(8,128)} reshape(f32[16,256,176]{2,1,0:T(8,128)} %bitcast.83) | data formatting | bytes 5767168 | tf_op jit(solution)/shard_map/concatenate | solution.py:106
  324.0 3.9 collective-permute-start.14
  327.9 29.8 %collective-permute-done.14 = f32[8,47872]{1,0:T(8,128)} collective-permute-done((f32[8,47872]{1,0:T(8,128)S(1)}, f32[8,47872]{1,0:T(8,128)}, u32[]{:S(2)}, u32[]{:S(2)}) %collective-permute-start.14) | collective-permute-done | bytes 1531936 | tf_op jit(solution)/shard_map/ppermute | solution.py:71
  361.4 2.2 dynamic-slice_bitcast_fusion.1
  363.5 2.2 collective-permute-start.15
  365.7 12.9 %collective-permute-done.15 = f32[4,47872]{1,0:T(4,128)} collective-permute-done((f32[4,47872]{1,0:T(4,128)}, f32[4,47872]{1,0:T(4,128)}, u32[]{:S(2)}, u32[]{:S(2)}) %collective-permute-start.15) | collective-permute-done | bytes 765984 | tf_op jit(solution)/shard_map/ppermute | solution.py:71
  378.6 2.2 bitcast_add_fusion.1
  382.6 9.5 %collective-permute-start.16 = (f32[2,47872]{1,0:T(2,128)S(1)}, f32[2,47872]{1,0:T(2,128)S(1)}, u32[]{:S(2)}, u32[]{:S(2)}) collective-permute-start(f32[2,47872]{1,0:T(2,128)S(1)} %dynamic-slice_bitcast_fusion.2), channel_id=1, source_target_pairs={{0,2},{1,3},{2,0},{3,1},{4,6},{5,7},{6,4},{7,5},{8,10},{9,11},{10,... | collective-permute-start | bytes 1148936 | tf_op jit(solution)/shard_map/ppermute | solution.py:71
  392.2 23.8 %collective-permute-done.16 = f32[2,47872]{1,0:T(2,128)S(1)} collective-permute-done((f32[2,47872]{1,0:T(2,128)S(1)}, f32[2,47872]{1,0:T(2,128)S(1)}, u32[]{:S(2)}, u32[]{:S(2)}) %collective-permute-start.16) | collective-permute-done | bytes 383008 | tf_op jit(solution)/shard_map/ppermute | solution.py:71
  418.3 10.4 %collective-permute-done.17 = f32[1,47872]{1,0:T(1,128)S(1)} collective-permute-done((f32[1,47872]{1,0:T(1,128)S(1)}, f32[1,47872]{1,0:T(1,128)S(1)}, u32[]{:S(2)}, u32[]{:S(2)}) %collective-permute-start.17) | collective-permute-done | bytes 191520 | tf_op jit(solution)/shard_map/ppermute | solution.py:71
  434.0 9.1 %collective-permute-done.18 = f32[16,4224]{1,0:T(8,128)} collective-permute-done((f32[16,4224]{1,0:T(8,128)}, f32[16,4224]{1,0:T(8,128)}, u32[]{:S(2)}, u32[]{:S(2)}) %collective-permute-start.18) | collective-permute-done | bytes 270368 | tf_op jit(solution)/shard_map/ppermute | solution.py:71
  448.4 2.3 copy.65
  451.7 2.2 collective-permute-start.20
  453.9 3.0 fusion.51
  458.4 3.1 copy.68
  461.6 17.3 %collective-permute-start.21 = (f32[2,4224]{1,0:T(2,128)S(1)}, f32[2,4224]{1,0:T(2,128)S(1)}, u32[]{:S(2)}, u32[]{:S(2)}) collective-permute-start(f32[2,4224]{1,0:T(2,128)S(1)} %dynamic-slice_bitcast_fusion.6), channel_id=1, source_target_pairs={{0,32},{16,48},{32,0},{48,16},{64,96},{80,112},{96,64},{112,80},{1... | collective-permute-start | bytes 101384 | tf_op jit(solution)/shard_map/ppermute | solution.py:71
  478.9 2.2 add_add_fusion
  485.0 6.3 %collective-permute-done.13 = f32[3,2816]{1,0:T(4,128)S(1)} collective-permute-done((f32[3,2816]{1,0:T(4,128)S(1)}, f32[3,2816]{1,0:T(4,128)S(1)}, u32[]{:S(2)}, u32[]{:S(2)}) %collective-permute-start.13) | collective-permute-done | bytes 33824 | tf_op jit(solution)/shard_map/ppermute | solution.py:13
  (152 shorter events, 70.4 us)
Async XLA Ops:
  50.4 25.6 %collective-permute-start = (bf16[1,520,176]{2,1,0:T(8,128)(2,1)S(1)}, bf16[1,520,176]{2,1,0:T(8,128)(2,1)S(1)}, u32[]{:S(2)}, u32[]{:S(2)}) collective-permute-start(bf16[1,520,176]{2,1,0:T(8,128)(2,1)S(1)} %bitcast.99), channel_id=1, source_target_pairs={{0,1},{1,0},{2,3},{3,2},{4,5},{5,4},{6,7},{7,6},{8,9},{9,8},{10,11... | collective-permute-start | bytes 549128 | tf_op jit(solution)/shard_map/ppermute | solution.py:71
  76.4 53.4 %collective-permute-start.1 = (bf16[2,520,176]{1,2,0:T(8,128)(2,1)S(1)}, bf16[2,520,176]{1,2,0:T(8,128)(2,1)S(1)}, u32[]{:S(2)}, u32[]{:S(2)}) collective-permute-start(bf16[2,520,176]{1,2,0:T(8,128)(2,1)S(1)} %copy.45), channel_id=1, source_target_pairs={{0,2},{1,3},{2,0},{3,1},{4,6},{5,7},{6,4},{7,5},{8,10},{9,11},{10,... | collective-permute-start | bytes 1098248 | tf_op jit(solution)/shard_map/ppermute | solution.py:71
  131.1 23.8 %collective-permute-start.2 = (bf16[4,520,176]{1,2,0:T(8,128)(2,1)S(1)}, bf16[4,520,176]{1,2,0:T(8,128)(2,1)S(1)}, u32[]{:S(2)}, u32[]{:S(2)}) collective-permute-start(bf16[4,520,176]{1,2,0:T(8,128)(2,1)S(1)} %copy.48), channel_id=1, source_target_pairs={{0,4},{1,5},{2,6},{3,7},{4,0},{5,1},{6,2},{7,3},{8,12},{9,13},{10,... | collective-permute-start | bytes 2196488 | tf_op jit(solution)/shard_map/ppermute | solution.py:71
  157.7 1.0 copy-start.8
  164.4 44.1 %collective-permute-start.3 = (bf16[8,520,176]{1,2,0:T(8,128)(2,1)}, bf16[8,520,176]{1,2,0:T(8,128)(2,1)}, u32[]{:S(2)}, u32[]{:S(2)}) collective-permute-start(bf16[8,520,176]{1,2,0:T(8,128)(2,1)} %copy.51), channel_id=1, source_target_pairs={{0,8},{1,9},{2,10},{3,11},{4,12},{5,13},{6,14},{7,15},{8,0},{9,1},... | collective-permute-start | bytes 4392968 | tf_op jit(solution)/shard_map/ppermute | solution.py:71
  168.6 10.6 %collective-permute-start.4 = (bf16[3,2816]{1,0:T(4,128)(2,1)S(1)}, bf16[3,2816]{1,0:T(4,128)(2,1)S(1)}, u32[]{:S(2)}, u32[]{:S(2)}) collective-permute-start(bf16[3,2816]{1,0:T(4,128)(2,1)S(1)} %slice_bitcast_fusion), channel_id=1, source_target_pairs={{0,1},{1,2},{2,3},{3,4},{4,5},{5,6},{6,7},{7,8},{8,9},{9,10},{10,1... | collective-permute-start | bytes 50696 | tf_op jit(solution)/shard_map/ppermute | solution.py:13
  219.4 1.1 copy-start.17
  223.5 3.3 copy-start
  228.6 2.6 copy-start.2
  228.8 2.4 copy-start.21
  231.2 1.1 copy-start.15
  232.3 1.2 copy-start.12
  247.8 1.1 copy-start.18
  249.9 9.8 %collective-permute-start.5 = (f32[2,2816]{1,0:T(2,128)S(1)}, f32[2,2816]{1,0:T(2,128)S(1)}, u32[]{:S(2)}, u32[]{:S(2)}) collective-permute-start(f32[2,2816]{1,0:T(2,128)S(1)} %get-tuple-element.45), channel_id=1, source_target_pairs={{1,0},{2,1},{3,2},{4,3},{5,4},{6,5},{7,6},{8,7},{9,8},{10,9},{11,1... | collective-permute-start | bytes 67592 | tf_op jit(solution)/shard_map/ppermute | solution.py:13
  251.9 10.5 %collective-permute-start.9 = (f32[2,2816]{1,0:T(2,128)S(1)}, f32[2,2816]{1,0:T(2,128)S(1)}, u32[]{:S(2)}, u32[]{:S(2)}) collective-permute-start(f32[2,2816]{1,0:T(2,128)S(1)} %get-tuple-element.44), channel_id=1, source_target_pairs={{0,1},{1,2},{2,3},{3,4},{4,5},{5,6},{6,7},{7,8},{8,9},{9,10},{10,1... | collective-permute-start | bytes 67592 | tf_op jit(solution)/shard_map/ppermute | solution.py:13
  263.4 15.5 %collective-permute-start.10 = (f32[2,2816]{1,0:T(2,128)S(1)}, f32[2,2816]{1,0:T(2,128)S(1)}, u32[]{:S(2)}, u32[]{:S(2)}) collective-permute-start(f32[2,2816]{1,0:T(2,128)S(1)} %pad_maximum_fusion.11), channel_id=1, source_target_pairs={{0,2},{1,3},{2,4},{3,5},{4,6},{5,7},{6,8},{7,9},{8,10},{9,11},{10,... | collective-permute-start | bytes 67592 | tf_op jit(solution)/shard_map/ppermute | solution.py:13
  269.9 14.4 %collective-permute-start.6 = (f32[2,2816]{1,0:T(2,128)S(1)}, f32[2,2816]{1,0:T(2,128)S(1)}, u32[]{:S(2)}, u32[]{:S(2)}) collective-permute-start(f32[2,2816]{1,0:T(2,128)S(1)} %pad_maximum_fusion.8), channel_id=1, source_target_pairs={{2,0},{3,1},{4,2},{5,3},{6,4},{7,5},{8,6},{9,7},{10,8},{11,9},{12,... | collective-permute-start | bytes 67592 | tf_op jit(solution)/shard_map/ppermute | solution.py:13
  279.0 8.9 %collective-permute-start.11 = (f32[2,2816]{1,0:T(2,128)S(1)}, f32[2,2816]{1,0:T(2,128)S(1)}, u32[]{:S(2)}, u32[]{:S(2)}) collective-permute-start(f32[2,2816]{1,0:T(2,128)S(1)} %pad_maximum_fusion.12), channel_id=1, source_target_pairs={{0,4},{1,5},{2,6},{3,7},{4,8},{5,9},{6,10},{7,11},{8,12},{9,13},{1... | collective-permute-start | bytes 67592 | tf_op jit(solution)/shard_map/ppermute | solution.py:13
  284.4 5.1 %collective-permute-start.7 = (f32[2,2816]{1,0:T(2,128)S(1)}, f32[2,2816]{1,0:T(2,128)S(1)}, u32[]{:S(2)}, u32[]{:S(2)}) collective-permute-start(f32[2,2816]{1,0:T(2,128)S(1)} %pad_maximum_fusion.9), channel_id=1, source_target_pairs={{4,0},{5,1},{6,2},{7,3},{8,4},{9,5},{10,6},{11,7},{12,8},{13,9},{1... | collective-permute-start | bytes 67592 | tf_op jit(solution)/shard_map/ppermute | solution.py:13
  288.0 7.7 %collective-permute-start.12 = (f32[2,2816]{1,0:T(2,128)S(1)}, f32[2,2816]{1,0:T(2,128)S(1)}, u32[]{:S(2)}, u32[]{:S(2)}) collective-permute-start(f32[2,2816]{1,0:T(2,128)S(1)} %pad_maximum_fusion.13), channel_id=1, source_target_pairs={{0,8},{1,9},{2,10},{3,11},{4,12},{5,13},{6,14},{7,15},{16,24},{17,... | collective-permute-start | bytes 67592 | tf_op jit(solution)/shard_map/ppermute | solution.py:13
  289.5 8.4 %collective-permute-start.8 = (f32[2,2816]{1,0:T(2,128)S(1)}, f32[2,2816]{1,0:T(2,128)S(1)}, u32[]{:S(2)}, u32[]{:S(2)}) collective-permute-start(f32[2,2816]{1,0:T(2,128)S(1)} %pad_maximum_fusion.10), channel_id=1, source_target_pairs={{8,0},{9,1},{10,2},{11,3},{12,4},{13,5},{14,6},{15,7},{24,16},{25,... | collective-permute-start | bytes 67592 | tf_op jit(solution)/shard_map/ppermute | solution.py:13
  295.8 2.2 copy-start.3
  295.8 2.7 copy-start.4
  295.8 3.1 copy-start.13
  305.9 1.5 copy-start.7
  307.5 2.2 copy-start.9
  322.4 1.6 copy-start.6
  324.0 33.7 %collective-permute-start.14 = (f32[8,47872]{1,0:T(8,128)S(1)}, f32[8,47872]{1,0:T(8,128)}, u32[]{:S(2)}, u32[]{:S(2)}) collective-permute-start(f32[8,47872]{1,0:T(8,128)S(1)} %dynamic-slice_bitcast_fusion), channel_id=1, source_target_pairs={{0,8},{1,9},{2,10},{3,11},{4,12},{5,13},{6,14},{7,15},{8,0},{9,1},... | collective-permute-start | bytes 4595720 | tf_op jit(solution)/shard_map/ppermute | solution.py:71
  361.4 17.3 %copy-start.11 = (f32[2,4,47872]{2,1,0:T(4,128)S(1)}, f32[2,4,47872]{2,1,0:T(4,128)}, u32[]{:S(2)}) copy-start(f32[2,4,47872]{2,1,0:T(4,128)} %reshape.141) | copy-start | bytes 4595716
  363.5 15.1 %collective-permute-start.15 = (f32[4,47872]{1,0:T(4,128)}, f32[4,47872]{1,0:T(4,128)}, u32[]{:S(2)}, u32[]{:S(2)}) collective-permute-start(f32[4,47872]{1,0:T(4,128)} %dynamic-slice_bitcast_fusion.1), channel_id=1, source_target_pairs={{0,4},{1,5},{2,6},{3,7},{4,0},{5,1},{6,2},{7,3},{8,12},{9,13},{10,... | collective-permute-start | bytes 2297864 | tf_op jit(solution)/shard_map/ppermute | solution.py:71
  382.6 33.3 %collective-permute-start.16 = (f32[2,47872]{1,0:T(2,128)S(1)}, f32[2,47872]{1,0:T(2,128)S(1)}, u32[]{:S(2)}, u32[]{:S(2)}) collective-permute-start(f32[2,47872]{1,0:T(2,128)S(1)} %dynamic-slice_bitcast_fusion.2), channel_id=1, source_target_pairs={{0,2},{1,3},{2,0},{3,1},{4,6},{5,7},{6,4},{7,5},{8,10},{9,11},{10,... | collective-permute-start | bytes 1148936 | tf_op jit(solution)/shard_map/ppermute | solution.py:71
  416.3 12.4 %collective-permute-start.17 = (f32[1,47872]{1,0:T(1,128)S(1)}, f32[1,47872]{1,0:T(1,128)S(1)}, u32[]{:S(2)}, u32[]{:S(2)}) collective-permute-start(f32[1,47872]{1,0:T(1,128)S(1)} %constant_dynamic-slice_fusion.1), channel_id=1, source_target_pairs={{0,1},{1,0},{2,3},{3,2},{4,5},{5,4},{6,7},{7,6},{8,9},{9,8},{10,11... | collective-permute-start | bytes 574472 | tf_op jit(solution)/shard_map/ppermute | solution.py:71
  429.5 17.2 %copy-start.1 = (bf16[256,16,176]{0,2,1:T(8,128)(2,1)S(1)}, bf16[256,16,176]{0,2,1:T(8,128)(2,1)}, u32[]{:S(2)}) copy-start(bf16[256,16,176]{0,2,1:T(8,128)(2,1)} %copy-done) | copy-start | bytes 4325380
  431.9 11.1 %collective-permute-start.18 = (f32[16,4224]{1,0:T(8,128)}, f32[16,4224]{1,0:T(8,128)}, u32[]{:S(2)}, u32[]{:S(2)}) collective-permute-start(f32[16,4224]{1,0:T(8,128)} %dynamic-slice_bitcast_fusion.3), channel_id=1, source_target_pairs={{0,256},{16,272},{32,288},{48,304},{64,320},{80,336},{96,352},{112... | collective-permute-start | bytes 811016 | tf_op jit(solution)/shard_map/ppermute | solution.py:71
  434.0 12.7 %copy-start.10 = (bf16[128,2816]{0,1:T(8,128)(2,1)S(1)}, bf16[128,2816]{0,1:T(8,128)(2,1)}, u32[]{:S(2)}) copy-start(bf16[128,2816]{0,1:T(8,128)(2,1)} %copy-done.9) | copy-start | bytes 2162692
  444.0 0.7 copy-start.19
  444.7 6.9 %collective-permute-start.19 = (f32[8,4224]{1,0:T(8,128)S(1)}, f32[8,4224]{1,0:T(8,128)S(1)}, u32[]{:S(2)}, u32[]{:S(2)}) collective-permute-start(f32[8,4224]{1,0:T(8,128)S(1)} %dynamic-slice_bitcast_fusion.4), channel_id=1, source_target_pairs={{0,128},{16,144},{32,160},{48,176},{64,192},{80,208},{96,224},{112... | collective-permute-start | bytes 405512 | tf_op jit(solution)/shard_map/ppermute | solution.py:71
  448.4 3.2 copy-start.20
  451.7 9.8 %collective-permute-start.20 = (f32[4,4224]{1,0:T(4,128)S(1)}, f32[4,4224]{1,0:T(4,128)S(1)}, u32[]{:S(2)}, u32[]{:S(2)}) collective-permute-start(f32[4,4224]{1,0:T(4,128)S(1)} %dynamic-slice_bitcast_fusion.5), channel_id=1, source_target_pairs={{0,64},{16,80},{32,96},{48,112},{64,0},{80,16},{96,32},{112,48},{1... | collective-permute-start | bytes 202760 | tf_op jit(solution)/shard_map/ppermute | solution.py:71
  453.9 3.0 copy-start.14
  458.4 20.5 %copy-start.5 = (f32[128,2816]{1,0:T(8,128)S(1)}, f32[128,2816]{1,0:T(8,128)}, u32[]{:S(2)}) copy-start(f32[128,2816]{1,0:T(8,128)} %copy.60) | copy-start | bytes 4325380
  458.4 20.5 %copy-start.16 = (f32[128,2816]{1,0:T(8,128)S(1)}, f32[128,2816]{1,0:T(8,128)}, u32[]{:S(2)}) copy-start(f32[128,2816]{1,0:T(8,128)} %copy.64) | copy-start | bytes 4325380
  461.6 21.4 %collective-permute-start.21 = (f32[2,4224]{1,0:T(2,128)S(1)}, f32[2,4224]{1,0:T(2,128)S(1)}, u32[]{:S(2)}, u32[]{:S(2)}) collective-permute-start(f32[2,4224]{1,0:T(2,128)S(1)} %dynamic-slice_bitcast_fusion.6), channel_id=1, source_target_pairs={{0,32},{16,48},{32,0},{48,16},{64,96},{80,112},{96,64},{112,80},{1... | collective-permute-start | bytes 101384 | tf_op jit(solution)/shard_map/ppermute | solution.py:71
  481.1 10.3 %collective-permute-start.13 = (f32[3,2816]{1,0:T(4,128)S(1)}, f32[3,2816]{1,0:T(4,128)S(1)}, u32[]{:S(2)}, u32[]{:S(2)}) collective-permute-start(f32[3,2816]{1,0:T(4,128)S(1)} %slice.236), channel_id=1, source_target_pairs={{1,0},{2,1},{3,2},{4,3},{5,4},{6,5},{7,6},{8,7},{9,8},{10,9},{11,1... | collective-permute-start | bytes 101384 | tf_op jit(solution)/shard_map/ppermute | solution.py:13
  483.1 9.8 %collective-permute-start.22 = (f32[1,4224]{1,0:T(1,128)S(1)}, f32[1,4224]{1,0:T(1,128)S(1)}, u32[]{:S(2)}, u32[]{:S(2)}) collective-permute-start(f32[1,4224]{1,0:T(1,128)S(1)} %constant_dynamic-slice_fusion), channel_id=1, source_target_pairs={{0,16},{16,0},{32,48},{48,32},{64,80},{80,64},{96,112},{112,96},{1... | collective-permute-start | bytes 50696 | tf_op jit(solution)/shard_map/ppermute | solution.py:71
